TPU v7x, 32 devices: a whole 2x2x4 slice. The times are simulated.
32 devices in a mesh: tract: 2 (over x), skyx: 4 (over y, core), skyy: 4 (over z).
Axes of the slice: x: 2, y: 2, z: 4, core: 2. Of those that a mesh axis runs over, the one named last changes fastest.
Arguments:
- images: bfloat16 [8, 8, 136, 4480], P(('tract', 'skyy'), 'skyx'), parts along dimension 0, may hold values from -6 to 6
- masks: int32 [8, 8, 136, 4480], P(('tract', 'skyy'), 'skyx'), parts along dimension 0, may hold values 0 or 1
- row_kernels: bfloat16 [8, 8, 128, 136], P(('tract', 'skyy'), 'skyx'), parts along dimension 0, may hold values from -1 to 2
- col_kernel: bfloat16 [66, 384, 128], P('tract'), parts along dimension 0, may hold values from -1 to 2
- inv_var: float32 [8, 8], P(('tract', 'skyy')), parts along dimension 0, may hold values from 0.5 to 4
- dest_col: int32 [8, 128, 1], P(('tract', 'skyy'), 'skyx'), parts along dimension 0, may hold values from 0 to 3; in each aligned block of 32 rows (0 to 31, 32 to 63, ..., all dimensions but the last counted through in order) at most 12 rows name the same one
- dest_row: int32 [8, 128], P(('tract', 'skyy'), 'skyx'), parts along dimension 0, may hold values from 0 to 31
Outputs:
- coadd: float32 [1024, 15872], P(('tract', 'skyy'), 'skyx'), parts along dimension 0
There are 2 independent parts, one for each index of `tract`. A program takes and returns all parts, laid end to end along the dimension named above; each array names one. Nothing has to cross between parts.
Inputs may be any that keep to these rules, and one draw needn't show every extreme that they name: `dest_col`: the 32 row blocks of any one device name one patch column at most 12 times, and some device names one exactly 12 times.
All inputs are finite; a program needn't handle non-finite values. No bound on the sum of `masks` on one device may be relied on, other than what follows from the above.
Results may differ from a plain program's by a relative error of at most 0.0057.
Values may be sent and summed in bfloat16 or wider, within the bound.
No kernel may reach another device: no remote copies, remote signals or barrier semaphores. Data moves between devices by JAX's collectives and lax.ppermute only.
A program may use at most 128 MiB of HBM per device.

v0:
```python
import jax
import jax.numpy as jnp
from jax import lax
from jax.sharding import PartitionSpec as P

PW = 3968
OVY = 64
PR = 128
RB = 8
CR = 256


def shifted(value, axis, steps):
    count = lax.axis_size(axis)
    first, last = (max(0, -steps), min(count, count - steps))
    return lax.ppermute(value, axis, [(source, source + steps) for source in range(first, last)])


def resample_columns(row_warped, col_kernel):
    tile_count = col_kernel.shape[0]
    tile_width = col_kernel.shape[2]
    full_span = tile_count * tile_width
    leading = row_warped.shape[:-1]
    summed = None
    for shift_tile in range(3):
        window = row_warped[..., shift_tile * tile_width : shift_tile * tile_width + full_span]
        window = window.reshape(leading + (tile_count, tile_width))
        kernel_part = col_kernel[:, shift_tile * tile_width : (shift_tile + 1) * tile_width, :]
        partial_sum = jnp.einsum(
            "...tk,tkj->...tj", window, kernel_part, preferred_element_type=jnp.float32
        )
        summed = partial_sum if summed is None else summed + partial_sum
    return summed.reshape(leading + (full_span,))


def place_rows(recv_blocks, recv_rows, positions):
    flat_blocks = recv_blocks.reshape((-1,) + recv_blocks.shape[2:])
    onehot_pos = (recv_rows.reshape(-1)[:, None] == jnp.arange(positions)[None, :]).astype(
        jnp.bfloat16
    )
    canvas = jnp.einsum(
        "sn,srpw->nrpw", onehot_pos, flat_blocks, preferred_element_type=jnp.float32
    )
    return canvas.reshape((positions * flat_blocks.shape[1],) + flat_blocks.shape[2:])


def local(images, masks, row_kernels, col_kernel, inv_var, dest_col, dest_row):
    exposures = images.shape[1]
    tile_width = col_kernel.shape[2]
    good_pix = (masks[0] == 0).astype(jnp.bfloat16)
    planes = jnp.stack([images[0] * good_pix, good_pix], axis=2)
    row_warped = jnp.einsum(
        "eqh,ehpw->eqpw", row_kernels[0], planes, preferred_element_type=jnp.float32
    ).astype(jnp.bfloat16)
    all_weights = inv_var[0]
    first_exp = lax.axis_index("skyx") * exposures
    slot_dest = dest_col[0, :, 0]
    slot_rows = dest_row[0]
    slot_count = slot_dest.shape[0]
    peers = lax.axis_size("skyx")
    capacity = max(2, (3 * slot_count + 2 * peers - 1) // (2 * peers))
    positions = CR // RB
    earlier = (jnp.arange(slot_count)[None, :] < jnp.arange(slot_count)[:, None]).astype(jnp.int32)
    onehot_dest = (slot_dest[:, None] == jnp.arange(peers)[None, :]).astype(jnp.int32)
    ranks = jnp.sum(jnp.dot(earlier, onehot_dest) * onehot_dest, axis=1)
    chosen = (slot_dest[None, None, :] == jnp.arange(peers)[:, None, None]) & (
        ranks[None, None, :] == jnp.arange(capacity)[None, :, None]
    )
    chosen_bf = chosen.astype(jnp.bfloat16)
    send_rows = jnp.sum(jnp.where(chosen, slot_rows[None, None, :] + 1, 0), axis=2) - 1
    weights = lax.dynamic_slice_in_dim(all_weights, first_exp, exposures)
    warped = resample_columns(row_warped, col_kernel)
    contribution = (weights[:, None, None, None] * warped).astype(jnp.bfloat16)
    blocks = contribution.reshape((slot_count, RB) + contribution.shape[2:])
    send_buf = jnp.einsum(
        "dcs,srpw->dcrpw", chosen_bf, blocks, preferred_element_type=jnp.float32
    ).astype(jnp.bfloat16)
    arrived, recv_rows = (
        lax.all_to_all(send_buf, "skyx", split_axis=0, concat_axis=0, tiled=True),
        lax.all_to_all(send_rows, "skyx", split_axis=0, concat_axis=0, tiled=True),
    )
    canvas = place_rows(arrived, recv_rows, positions)
    from_left = shifted(canvas[:, :, tile_width + PW :], "skyx", 1)
    from_right = shifted(canvas[:, :, :tile_width], "skyx", -1)
    inner_part = canvas[:, :, tile_width : tile_width + PW]
    inner_part = inner_part.at[:, :, :tile_width].add(from_left)
    inner_part = inner_part.at[:, :, PW - tile_width :].add(from_right)
    from_above = shifted(inner_part[OVY + PR :], "skyy", 1)
    from_below = shifted(inner_part[:OVY], "skyy", -1)
    interior = inner_part[OVY : OVY + PR]
    interior = interior.at[:OVY].add(from_above)
    interior = interior.at[PR - OVY :].add(from_below)
    return interior[:, 0, :] / jnp.maximum(interior[:, 1, :], 1.0)


def solution(mesh):
    in_specs = (
        P(("tract", "skyy"), "skyx", None, None),
        P(("tract", "skyy"), "skyx", None, None),
        P(("tract", "skyy"), "skyx", None, None),
        P("tract", None, None),
        P(("tract", "skyy"), None),
        P(("tract", "skyy"), "skyx", None),
        P(("tract", "skyy"), "skyx"),
    )
    out_specs = P(("tract", "skyy"), "skyx")
    return jax.shard_map(local, mesh=mesh, in_specs=in_specs, out_specs=out_specs, check_vma=False)
```

profile of v0, /device:TPU:1, one launch (start us, length us, event | category | flops | bytes accessed | tf_op | source)
XLA Modules:
  0.0 228.0 jit_solution(11657109731242041013)
XLA Ops:
  2.9 4.3 %all-to-all-start = ((s32[4,1,12]{2,1,0:T(1,128)}), s32[4,1,12]{2,1,0:T(1,128)S(1)}, u32[]{:S(2)}, u32[]{:S(2)}) async-start(s32[4,1,12]{2,1,0:T(1,128)} %bitcast.3), calls=%async_computation | async-start | bytes 4096 | tf_op jit(solution)/shard_map/all_to_all | solution.py:80
  7.2 4.3 %select_bitcast_fusion = (bf16[2,136,1,4480]{3,1,2,0:T(8,128)(2,1)S(1)}, pred[1,2,136,4480]{3,2,1,0:T(8,128)(4,1)S(1)}) fusion(bf16[1,2,136,4480]{3,2,1,0:T(8,128)(2,1)} %param.15, s32[1,2,136,4480]{3,2,1,0:T(8,128)} %param.16), kind=kLoop, calls=%fused_computation.20 | loop fusion | flops 2437120 | bytes 10967040 | tf_op jit(solution)/shard_map/mul | solution.py:51
  11.7 3.7 %fusion = bf16[2,128,2,4480]{1,3,2,0:T(8,128)(2,1)S(1)} fusion(bf16[2,136,1,4480]{3,1,2,0:T(8,128)(2,1)S(1)} %convert_bitcast_fusion, bf16[2,136,1,4480]{3,1,2,0:T(8,128)(2,1)S(1)} %get-tuple-element.53, bf16[1,2,128,136]{2,3,1,0:T(8,128)(2,1)S(1)} %copy-done), kind=kOutput, calls=%fused_computation.5 | convolution fusion | flops 628633600 | bytes 9531392 | tf_op jit(solution)/shard_map/eqh,ehpw->eqpw/dot_general | solution.py:52
  15.4 3.8 %fusion.41 = (bf16[2,128,2,4224]{1,3,2,0:T(8,128)(2,1)}, bf16[2,128,2,4224]{1,3,2,0:T(8,128)(2,1)}, bf16[2,128,2,4224]{1,3,2,0:T(8,128)(2,1)S(1)}) fusion(bf16[2,128,2,4480]{1,3,2,0:T(8,128)(2,1)S(1)} %fusion), kind=kLoop, calls=%fused_computation.62 | loop fusion | bytes 25952256 | tf_op jit(solution)/shard_map/slice | solution.py:26
  19.2 3.9 %fusion.7 = f32[33,2,128,2,128]{4,2,3,1,0:T(8,128)S(1)} fusion(bf16[2,128,2,33,128]{1,4,3,2,0:T(8,128)(2,1)} %bitcast.68, bf16[33,384,128]{2,1,0:T(8,128)(2,1)} %param.18), kind=kOutput, calls=%fused_computation.12 | convolution fusion | flops 553648128 | bytes 14057472 | tf_op jit(solution)/shard_map/...tk,tkj->...tj/dot_general | solution.py:29
  23.1 6.0 %fusion.9 = f32[33,2,128,2,128]{4,2,3,1,0:T(8,128)} fusion(bf16[2,128,2,33,128]{1,4,3,2,0:T(8,128)(2,1)S(1)} %bitcast.67, bf16[33,384,128]{2,1,0:T(8,128)(2,1)} %param.18), kind=kOutput, calls=%fused_computation.14 | convolution fusion | flops 553648128 | bytes 14057472 | tf_op jit(solution)/shard_map/...tk,tkj->...tj/dot_general | solution.py:29
  29.1 10.3 %add_bitcast_fusion = f32[2,128,2,33,128]{4,1,2,0,3:T(8,128)} fusion(f32[33,2,128,2,128]{4,2,3,1,0:T(8,128)S(1)} %fusion.7, f32[33,2,128,2,128]{4,2,3,1,0:T(8,128)} %fusion.9, bf16[2,128,2,33,128]{1,4,3,2,0:T(8,128)(2,1)} %bitcast.66, bf16[33,384,128]{2,1,0:T(8,128)(2,1)} %param.18), kind=kOutput, calls=%fused_computation.3 | convolution fusion | flops 557973504 | bytes 31358976 | tf_op jit(solution)/shard_map/...tk,tkj->...tj/dot_general | solution.py:29
  39.3 12.5 %copy.26 = f32[2,128,2,33,128]{4,3,1,0,2:T(8,128)} copy(f32[2,128,2,33,128]{4,1,2,0,3:T(8,128)} %add_bitcast_fusion) | data formatting | bytes 17301504 | tf_op jit(solution)/shard_map/add | solution.py:32
  51.9 9.8 %reshape.252 = f32[32,8,2,4224]{3,1,0,2:T(8,128)} reshape(f32[2,128,2,33,128]{4,3,1,0,2:T(8,128)} %copy.26) | data formatting | bytes 17301504 | tf_op jit(solution)/shard_map/reshape | solution.py:33
  61.9 4.1 %multiply_convert_fusion = bf16[32,8,2,4224]{3,1,0,2:T(8,128)(2,1)S(1)} fusion(f32[32,8,2,4224]{3,1,0,2:T(8,128)} %reshape.252, f32[32]{0:T(128)S(1)} %mul.30), kind=kLoop, calls=%fused_computation.2 | loop fusion | flops 4325376 | bytes 12976256 | tf_op jit(solution)/shard_map/convert_element_type | solution.py:73
  66.1 2.4 %convolution_convert_fusion = bf16[4,12,8,2,4224]{4,1,3,2,0:T(8,128)(2,1)S(1)} fusion(bf16[32,8,2,4224]{3,1,0,2:T(8,128)(2,1)S(1)} %multiply_convert_fusion, pred[12,32]{1,0:T(8,128)(4,1)S(1)} %iota_compare_fusion.3, pred[4,32]{1,0:T(4,128)(4,1)S(1)} %iota_compare_fusion.5), kind=kOutput, calls=%fused_computation | convolution fusion | flops 210863616 | bytes 10813952 | tf_op jit(solution)/shard_map/dcs,srpw->dcrpw/dot_general | solution.py:75
  68.5 4.7 %copy.28 = bf16[4,12,8,2,4224]{4,2,3,1,0:T(8,128)(2,1)} copy(bf16[4,12,8,2,4224]{4,1,3,2,0:T(8,128)(2,1)S(1)} %convolution_convert_fusion) | data formatting | bytes 12976128 | tf_op jit(solution)/shard_map/convert_element_type | solution.py:77
  73.1 5.3 %all-to-all-start.1 = ((bf16[4,12,8,2,4224]{4,2,3,1,0:T(8,128)(2,1)}), bf16[4,12,8,2,4224]{4,2,3,1,0:T(8,128)(2,1)}, u32[]{:S(2)}, u32[]{:S(2)}) async-start(bf16[4,12,8,2,4224]{4,2,3,1,0:T(8,128)(2,1)} %copy.28), calls=%async_computation.1 | async-start | bytes 12976128 | tf_op jit(solution)/shard_map/all_to_all | solution.py:79
  79.7 70.5 %all-to-all-done.1 = bf16[4,12,8,2,4224]{4,2,3,1,0:T(8,128)(2,1)} async-done(((bf16[4,12,8,2,4224]{4,2,3,1,0:T(8,128)(2,1)}), bf16[4,12,8,2,4224]{4,2,3,1,0:T(8,128)(2,1)}, u32[]{:S(2)}, u32[]{:S(2)}) %all-to-all-start.1) | async-done | bytes 6488096 | tf_op jit(solution)/shard_map/all_to_all | solution.py:79
  150.2 8.2 %fusion.1 = f32[32,8,2,4224]{3,0,2,1:T(8,128)} fusion(bf16[48,8,2,4224]{3,1,2,0:T(8,128)(2,1)} %bitcast.27, s32[48]{0:T(128)S(1)} %eq.94), kind=kOutput, calls=%fused_computation.6 | convolution fusion | flops 207619584 | bytes 15139008 | tf_op jit(solution)/shard_map/sn,srpw->nrpw/dot_general | solution.py:41
  158.4 8.5 %copy.58 = f32[32,8,2,4224]{3,1,0,2:T(8,128)S(1)} copy(f32[32,8,2,4224]{3,0,2,1:T(8,128)} %fusion.1) | data formatting | bytes 17301504 | tf_op jit(solution)/shard_map/sn,srpw->nrpw/dot_general | solution.py:41
  166.9 2.9 %collective-permute-start = (f32[256,2,128]{2,0,1:T(8,128)S(1)}, f32[256,2,128]{2,0,1:T(8,128)S(1)}, u32[]{:S(2)}, u32[]{:S(2)}) collective-permute-start(f32[256,2,128]{2,0,1:T(8,128)S(1)} %get-tuple-element.56), channel_id=1, source_target_pairs={{0,4},{4,8},{8,12},{1,5},{5,9},{9,13},{2,6},{6,10},{10,14},{3,7},{... | collective-permute-start | bytes 786440 | tf_op jit(solution)/shard_map/ppermute | solution.py:16
  169.9 1.9 collective-permute-start.1
  173.2 4.4 %collective-permute-done.1 = f32[256,2,128]{2,0,1:T(8,128)S(1)} collective-permute-done((f32[256,2,128]{2,0,1:T(8,128)S(1)}, f32[256,2,128]{2,0,1:T(8,128)S(1)}, u32[]{:S(2)}, u32[]{:S(2)}) %collective-permute-start.1) | collective-permute-done | bytes 262176 | tf_op jit(solution)/shard_map/ppermute | solution.py:16
  177.9 3.8 %collective-permute-start.2 = (f32[64,2,3968]{2,0,1:T(8,128)S(1)}, f32[64,2,3968]{2,0,1:T(8,128)S(1)}, u32[]{:S(2)}, u32[]{:S(2)}) collective-permute-start(f32[64,2,3968]{2,0,1:T(8,128)S(1)} %get-tuple-element.58), channel_id=1, source_target_pairs={{0,1},{1,2},{2,3},{4,5},{5,6},{6,7},{8,9},{9,10},{10,11},{12,13},{... | collective-permute-start | bytes 6094856 | tf_op jit(solution)/shard_map/ppermute | solution.py:16
  181.7 1.3 collective-permute-start.3
  183.3 38.5 %collective-permute-done.2 = f32[64,2,3968]{2,0,1:T(8,128)S(1)} collective-permute-done((f32[64,2,3968]{2,0,1:T(8,128)S(1)}, f32[64,2,3968]{2,0,1:T(8,128)S(1)}, u32[]{:S(2)}, u32[]{:S(2)}) %collective-permute-start.2) | collective-permute-done | bytes 2031648 | tf_op jit(solution)/shard_map/ppermute | solution.py:16
  222.1 4.0 %collective-permute-done.3 = f32[64,2,3968]{2,0,1:T(8,128)S(1)} collective-permute-done((f32[64,2,3968]{2,0,1:T(8,128)S(1)}, f32[64,2,3968]{2,0,1:T(8,128)S(1)}, u32[]{:S(2)}, u32[]{:S(2)}) %collective-permute-start.3) | collective-permute-done | bytes 2031648 | tf_op jit(solution)/shard_map/ppermute | solution.py:16
  226.4 1.6 fusion.17
  (29 shorter events, 7.3 us)
Async XLA Ops:
  0.0 11.7 %copy-start = (bf16[1,2,128,136]{2,3,1,0:T(8,128)(2,1)S(1)}, bf16[1,2,128,136]{2,3,1,0:T(8,128)(2,1)}, u32[]{:S(2)}) copy-start(bf16[1,2,128,136]{2,3,1,0:T(8,128)(2,1)} %param.17) | copy-start | bytes 208900
  2.9 70.2 %all-to-all-start = ((s32[4,1,12]{2,1,0:T(1,128)}), s32[4,1,12]{2,1,0:T(1,128)S(1)}, u32[]{:S(2)}, u32[]{:S(2)}) async-start(s32[4,1,12]{2,1,0:T(1,128)} %bitcast.3), calls=%async_computation | async-start | bytes 4096 | tf_op jit(solution)/shard_map/all_to_all | solution.py:80
  51.9 9.8 %copy-start.2 = (f32[1,8]{1,0:T(1,128)S(1)}, f32[1,8]{1,0:T(1,128)}, u32[]{:S(2)}) copy-start(f32[1,8]{1,0:T(1,128)} %param.19) | copy-start | bytes 100
  73.1 77.1 %all-to-all-start.1 = ((bf16[4,12,8,2,4224]{4,2,3,1,0:T(8,128)(2,1)}), bf16[4,12,8,2,4224]{4,2,3,1,0:T(8,128)(2,1)}, u32[]{:S(2)}, u32[]{:S(2)}) async-start(bf16[4,12,8,2,4224]{4,2,3,1,0:T(8,128)(2,1)} %copy.28), calls=%async_computation.1 | async-start | bytes 12976128 | tf_op jit(solution)/shard_map/all_to_all | solution.py:79
  166.9 6.2 %collective-permute-start = (f32[256,2,128]{2,0,1:T(8,128)S(1)}, f32[256,2,128]{2,0,1:T(8,128)S(1)}, u32[]{:S(2)}, u32[]{:S(2)}) collective-permute-start(f32[256,2,128]{2,0,1:T(8,128)S(1)} %get-tuple-element.56), channel_id=1, source_target_pairs={{0,4},{4,8},{8,12},{1,5},{5,9},{9,13},{2,6},{6,10},{10,14},{3,7},{... | collective-permute-start | bytes 786440 | tf_op jit(solution)/shard_map/ppermute | solution.py:16
  169.9 7.7 %collective-permute-start.1 = (f32[256,2,128]{2,0,1:T(8,128)S(1)}, f32[256,2,128]{2,0,1:T(8,128)S(1)}, u32[]{:S(2)}, u32[]{:S(2)}) collective-permute-start(f32[256,2,128]{2,0,1:T(8,128)S(1)} %get-tuple-element.55), channel_id=1, source_target_pairs={{4,0},{8,4},{12,8},{5,1},{9,5},{13,9},{6,2},{10,6},{14,10},{7,3},{... | collective-permute-start | bytes 786440 | tf_op jit(solution)/shard_map/ppermute | solution.py:16
  177.9 43.9 %collective-permute-start.2 = (f32[64,2,3968]{2,0,1:T(8,128)S(1)}, f32[64,2,3968]{2,0,1:T(8,128)S(1)}, u32[]{:S(2)}, u32[]{:S(2)}) collective-permute-start(f32[64,2,3968]{2,0,1:T(8,128)S(1)} %get-tuple-element.58), channel_id=1, source_target_pairs={{0,1},{1,2},{2,3},{4,5},{5,6},{6,7},{8,9},{9,10},{10,11},{12,13},{... | collective-permute-start | bytes 6094856 | tf_op jit(solution)/shard_map/ppermute | solution.py:16
  181.7 44.3 %collective-permute-start.3 = (f32[64,2,3968]{2,0,1:T(8,128)S(1)}, f32[64,2,3968]{2,0,1:T(8,128)S(1)}, u32[]{:S(2)}, u32[]{:S(2)}) collective-permute-start(f32[64,2,3968]{2,0,1:T(8,128)S(1)} %get-tuple-element.57), channel_id=1, source_target_pairs={{1,0},{2,1},{3,2},{5,4},{6,5},{7,6},{9,8},{10,9},{11,10},{13,12},{... | collective-permute-start | bytes 6094856 | tf_op jit(solution)/shard_map/ppermute | solution.py:16
  226.0 2.0 copy-start.1
where the time goes:
time: 229 us; the launch traced here: 228 us
  waiting for transfers between devices  118 us (52%)
  local copies, waits for them, and re-layouts  41.2 us (18%)
  matrix products  35.4 us (15%)
  starting transfers between devices  19.5 us (9%)
  other arithmetic  13.6 us (6%)
    all_to_all x1, waiting for transfers between devices, local(): lax.all_to_all(send_buf, 'skyx', split_axis=0, concat_axis=0, tiled=True)  70.5 us
    ppermute x4, waiting for transfers between devices, shifted(): lax.ppermute(value, axis, [(source, source + steps) for source in range(f...  47.7 us
    dot_general x3, matrix products, resample_columns(): jnp.einsum('...tk,tkj->...tj', window, kernel_part, preferred_element_typ...  20.2 us
    add x1, local copies, waits for them, and re-layouts, resample_columns(): summed = partial_sum if summed is None else summed + partial_sum  12.5 us
    ppermute x4, starting transfers between devices, shifted(): lax.ppermute(value, axis, [(source, source + steps) for source in range(f...  9.93 us
    reshape x1, local copies, waits for them, and re-layouts, resample_columns(): return summed.reshape(leading + (full_span,))  9.79 us
    dot_general x1, local copies, waits for them, and re-layouts, place_rows(): jnp.einsum('sn,srpw->nrpw', onehot_pos, flat_blocks, preferred_element_ty...  8.46 us
    dot_general x1, matrix products, place_rows(): jnp.einsum('sn,srpw->nrpw', onehot_pos, flat_blocks, preferred_element_ty...  8.22 us
  transfers between devices with their start and end apart: 6, of which 5 were waited for; matrix products, arithmetic and copies ran while one was open for 30% of the time, Pallas kernels for 0%

commit v1 on v0

v1 whole, which is shorter than its diff:
```python
import jax
import jax.numpy as jnp
from jax import lax
from jax.experimental import pallas as pl
from jax.experimental.pallas import tpu as pltpu
from jax.sharding import PartitionSpec as P

OVY = 64
PR = 128
RB = 8
ROW_CHUNK = 640


def shifted(value, axis, steps):
    count = lax.axis_size(axis)
    first, last = (max(0, -steps), min(count, count - steps))
    return lax.ppermute(value, axis, [(source, source + steps) for source in range(first, last)])


def warp_kernel(w_ref, img_ref, mask_ref, rk_ref, ck_ref, out_ref, rw_ref):
    e = pl.program_id(0)
    ph = rk_ref.shape[2]
    win = img_ref.shape[3]
    tiles, kw, tw = ck_ref.shape
    rk = rk_ref[0, 0]
    for c in range(win // ROW_CHUNK):
        cols = pl.ds(c * ROW_CHUNK, ROW_CHUNK)
        good = mask_ref[0, 0, :, cols] == 0
        img = img_ref[0, 0, :, cols]
        p0 = jnp.where(good, img, jnp.zeros_like(img))
        p1 = good.astype(jnp.bfloat16)
        rw_ref[0:ph, cols] = jnp.dot(rk, p0, preferred_element_type=jnp.float32).astype(jnp.bfloat16)
        rw_ref[ph : 2 * ph, cols] = jnp.dot(rk, p1, preferred_element_type=jnp.float32).astype(jnp.bfloat16)
    weight = w_ref[e]
    blocks = ph // RB

    def tile(t, carry):
        off = pl.multiple_of(t * tw, tw)
        x = rw_ref[:, pl.ds(off, kw)]
        r = jnp.dot(x, ck_ref[t], preferred_element_type=jnp.float32) * weight
        out_ref[:, 0, :, pl.ds(off, tw)] = r[0:ph].reshape(blocks, RB, tw).astype(jnp.bfloat16)
        out_ref[:, 1, :, pl.ds(off, tw)] = r[ph : 2 * ph].reshape(blocks, RB, tw).astype(jnp.bfloat16)
        return carry

    lax.fori_loop(0, tiles, tile, 0)


def warp(weights, images, masks, row_kernels, col_kernel):
    _, exposures, hin, win = images.shape
    ph = row_kernels.shape[2]
    tiles, kw, tw = col_kernel.shape
    cw = tiles * tw
    blocks = ph // RB
    return pl.pallas_call(
        warp_kernel,
        grid=(exposures,),
        in_specs=[
            pl.BlockSpec(memory_space=pltpu.SMEM),
            pl.BlockSpec((1, 1, hin, win), lambda e: (0, e, 0, 0)),
            pl.BlockSpec((1, 1, hin, win), lambda e: (0, e, 0, 0)),
            pl.BlockSpec((1, 1, ph, hin), lambda e: (0, e, 0, 0)),
            pl.BlockSpec((tiles, kw, tw), lambda e: (0, 0, 0)),
        ],
        out_specs=pl.BlockSpec((blocks, 2, RB, cw), lambda e: (e, 0, 0, 0)),
        out_shape=jax.ShapeDtypeStruct((exposures * blocks, 2, RB, cw), jnp.bfloat16),
        scratch_shapes=[pltpu.VMEM((2 * ph, win), jnp.bfloat16)],
        compiler_params=pltpu.CompilerParams(vmem_limit_bytes=56 * 1024 * 1024),
    )(weights, images, masks, row_kernels, col_kernel)


def local(images, masks, row_kernels, col_kernel, inv_var, dest_col, dest_row):
    exposures = images.shape[1]
    tile_width = col_kernel.shape[2]
    cw = col_kernel.shape[0] * tile_width
    pw = cw - 2 * tile_width
    first_exp = lax.axis_index("skyx") * exposures
    weights = lax.dynamic_slice_in_dim(inv_var[0], first_exp, exposures)
    blocks = warp(weights, images, masks, row_kernels, col_kernel)

    slot_dest = dest_col[0, :, 0]
    slot_rows = dest_row[0]
    slot_count = slot_dest.shape[0]
    peers = lax.axis_size("skyx")
    capacity = max(2, (3 * slot_count + 2 * peers - 1) // (2 * peers))
    positions = (PR + 2 * OVY) // RB
    earlier = (jnp.arange(slot_count)[None, :] < jnp.arange(slot_count)[:, None]).astype(jnp.int32)
    onehot_dest = (slot_dest[:, None] == jnp.arange(peers)[None, :]).astype(jnp.int32)
    ranks = jnp.sum(jnp.dot(earlier, onehot_dest) * onehot_dest, axis=1)
    chosen = (slot_dest[None, None, :] == jnp.arange(peers)[:, None, None]) & (
        ranks[None, None, :] == jnp.arange(capacity)[None, :, None]
    )
    send_rows = jnp.sum(jnp.where(chosen, slot_rows[None, None, :] + 1, 0), axis=2) - 1
    send_idx = jnp.sum(jnp.where(chosen, jnp.arange(slot_count)[None, None, :] + 1, 0), axis=2) - 1
    send_idx = jnp.where(send_idx < 0, slot_count, send_idx)
    send_buf = jnp.take(blocks, send_idx.reshape(-1), axis=0, mode="fill", fill_value=0)
    send_buf = send_buf.reshape((peers, capacity) + blocks.shape[1:])
    arrived = lax.all_to_all(send_buf, "skyx", split_axis=0, concat_axis=0, tiled=True)
    recv_rows = lax.all_to_all(send_rows, "skyx", split_axis=0, concat_axis=0, tiled=True)
    arrived = arrived.reshape((-1,) + blocks.shape[1:])
    onehot_pos = (recv_rows.reshape(-1)[:, None] == jnp.arange(positions)[None, :]).astype(jnp.bfloat16)
    canvas = jnp.einsum("sn,sprw->nprw", onehot_pos, arrived, preferred_element_type=jnp.float32)

    margin = OVY // RB
    inner = PR // RB
    upper = canvas[:margin].astype(jnp.bfloat16)
    lower = canvas[margin + inner :].astype(jnp.bfloat16)
    from_above = shifted(lower, "skyy", 1).astype(jnp.float32)
    from_below = shifted(upper, "skyy", -1).astype(jnp.float32)
    interior = canvas[margin : margin + inner]
    interior = interior.at[:margin].add(from_above)
    interior = interior.at[inner - margin :].add(from_below)

    left_part = interior[..., :tile_width].astype(jnp.bfloat16)
    right_part = interior[..., tile_width + pw :].astype(jnp.bfloat16)
    from_left = shifted(right_part, "skyx", 1).astype(jnp.float32)
    from_right = shifted(left_part, "skyx", -1).astype(jnp.float32)
    core = interior[..., tile_width : tile_width + pw]
    core = core.at[..., :tile_width].add(from_left)
    core = core.at[..., pw - tile_width :].add(from_right)
    num = core[:, 0].reshape(PR, pw)
    den = core[:, 1].reshape(PR, pw)
    return num / jnp.maximum(den, 1.0)


def solution(mesh):
    in_specs = (
        P(("tract", "skyy"), "skyx", None, None),
        P(("tract", "skyy"), "skyx", None, None),
        P(("tract", "skyy"), "skyx", None, None),
        P("tract", None, None),
        P(("tract", "skyy"), None),
        P(("tract", "skyy"), "skyx", None),
        P(("tract", "skyy"), "skyx"),
    )
    out_specs = P(("tract", "skyy"), "skyx")
    return jax.shard_map(local, mesh=mesh, in_specs=in_specs, out_specs=out_specs, check_vma=False)
```

time: 229 us -> 170 us (0.74)
  matrix products: 35.4 us -> 5.91 us
  local copies, waits for them, and re-layouts: 41.2 us -> 13.5 us
  Pallas kernels: 0 us -> 20.3 us
  waiting for transfers between devices: 118 us -> 98.4 us
  other arithmetic: 13.6 us -> 9.83 us
    dot_general x6 -> x1, matrix products: 34.5 us -> 5.04 us  [local(): jnp.einsum('sn,sprw->nprw', onehot_pos, arrived, preferred_element_type=j...]
    pallas_call x0 -> x1, Pallas kernels: none -> 20.3 us  [warp(): pl.pallas_call(warp_kernel, grid=(exposures,), in_specs=[pl.BlockSpec(mem...]
    ppermute x4, waiting for transfers between devices: 47.7 us -> 27.9 us  [shifted(): lax.ppermute(value, axis, [(source, source + steps) for source in range(f...]
    add x1 -> x0, local copies, waits for them, and re-layouts: 12.5 us -> none  [resample_columns(): summed = partial_sum if summed is None else summed + partial_sum]
    reshape x1 -> x0, local copies, waits for them, and re-layouts: 9.79 us -> none  [resample_columns(): return summed.reshape(leading + (full_span,))]
    dot_general x1 -> x0, local copies, waits for them, and re-layouts: 8.46 us -> none  [place_rows(): jnp.einsum('sn,srpw->nrpw', onehot_pos, flat_blocks, preferred_element_ty...]
    gather x0 -> x1, local copies, waits for them, and re-layouts: none -> 7.23 us  [local(): jnp.take(blocks, send_idx.reshape(-1), axis=0, mode='fill', fill_value=0)]
    select_n x0 -> x2, other arithmetic: none -> 6.18 us  [local(): jnp.take(blocks, send_idx.reshape(-1), axis=0, mode='fill', fill_value=0)]
  transfers between devices with their start and end apart: 6 -> 6, of which waited for: 5 -> 4; matrix products, arithmetic and copies ran while one was open for 30% -> 11% of each run, Pallas kernels for 0% -> 12%
where the time goes in v1:
time: 170 us; the launch traced here: 169 us
  waiting for transfers between devices  98.4 us (58%)
  starting transfers between devices  20.9 us (12%)
  Pallas kernels  20.3 us (12%)
  local copies, waits for them, and re-layouts  13.5 us (8%)
  other arithmetic  9.83 us (6%)
  matrix products  5.91 us (3%)
    all_to_all x1, waiting for transfers between devices, local(): lax.all_to_all(send_buf, 'skyx', split_axis=0, concat_axis=0, tiled=True)  70.5 us
    ppermute x4, waiting for transfers between devices, shifted(): lax.ppermute(value, axis, [(source, source + steps) for source in range(f...  27.9 us
    pallas_call x1, Pallas kernels, warp(): pl.pallas_call(warp_kernel, grid=(exposures,), in_specs=[pl.BlockSpec(mem...  20.3 us
    ppermute x4, starting transfers between devices, shifted(): lax.ppermute(value, axis, [(source, source + steps) for source in range(f...  11.3 us
    gather x1, local copies, waits for them, and re-layouts, local(): jnp.take(blocks, send_idx.reshape(-1), axis=0, mode='fill', fill_value=0)  7.23 us
    select_n x2, other arithmetic, local(): jnp.take(blocks, send_idx.reshape(-1), axis=0, mode='fill', fill_value=0)  6.18 us
    all_to_all x1, starting transfers between devices, local(): lax.all_to_all(send_buf, 'skyx', split_axis=0, concat_axis=0, tiled=True)  5.35 us
    dot_general x1, matrix products, local(): jnp.einsum('sn,sprw->nprw', onehot_pos, arrived, preferred_element_type=j...  5.04 us
  transfers between devices with their start and end apart: 6, of which 4 were waited for; matrix products, arithmetic and copies ran while one was open for 11% of the time, Pallas kernels for 12%

profile of v1, /device:TPU:1, one launch (start us, length us, event | category | flops | bytes accessed | tf_op | source)
XLA Modules:
  0.0 169.0 jit_solution(454121805507716710)
XLA Ops:
  0.0 0.9 fusion.5
  0.9 0.7 iota_compare_fusion.5
  1.5 0.7 add_bitcast_fusion
  2.2 0.5 fusion.8
  2.7 0.6 copy.31
  3.3 4.3 %all-to-all-start = ((s32[4,1,12]{2,1,0:T(1,128)}), s32[4,1,12]{2,1,0:T(1,128)S(1)}, u32[]{:S(2)}, u32[]{:S(2)}) async-start(s32[4,1,12]{2,1,0:T(1,128)} %bitcast.3), calls=%async_computation | async-start | bytes 4096 | tf_op jit(solution)/shard_map/all_to_all | solution.py:98
  7.8 1.7 copy.27.rk_ref
  9.5 0.6 fusion.14.w_ref
  10.1 20.3 %shard_map.73 = bf16[32,2,8,4224]{3,2,1,0:T(8,128)(2,1)} custom-call(f32[2]{0:T(128)} %fusion.14.w_ref, bf16[1,2,136,4480]{3,2,1,0:T(8,128)(2,1)} %img_ref.1, s32[1,2,136,4480]{3,2,1,0:T(8,128)} %mask_ref.1, bf16[1,2,128,136]{3,2,1,0:T(8,128)(2,1)} %copy.27.rk_ref, bf16[33,384,128]{2,1,0:T(8,128)(2,1)} %ck_ref.1), custom_call_target="tpu_custom_call" | custom-call | tf_op jit(solution)/shard_map/pallas_call | solution.py:54
  30.3 7.2 %gather_fusion = bf16[48,2,8,4224]{3,2,1,0:T(8,128)(2,1)} fusion(bf16[32,2,8,4224]{3,2,1,0:T(8,128)(2,1)} %shard_map.73, s32[1024]{0:T(1024)S(1)} %pad_clamp_fusion), kind=kCustom, calls=%fused_computation | custom fusion | bytes 12976320 | tf_op jit(solution)/shard_map/jit(_take)/gather | solution.py:95
  37.6 6.2 %broadcast_select_fusion = bf16[4,12,2,8,4224]{4,3,2,1,0:T(8,128)(2,1)} fusion(bf16[4,12,2,8,4224]{4,3,2,1,0:T(8,128)(2,1)} %bitcast.22, pred[4,12]{1,0:T(4,128)(4,1)S(1)} %compare_and_fusion), kind=kLoop, calls=%fused_computation.3 | loop fusion | flops 3244032 | bytes 12976176 | tf_op jit(solution)/shard_map/jit(_take)/select_n | solution.py:95
  43.7 5.4 %all-to-all-start.1 = ((bf16[4,12,2,8,4224]{4,3,2,1,0:T(8,128)(2,1)}), bf16[4,12,2,8,4224]{4,3,2,1,0:T(8,128)(2,1)}, u32[]{:S(2)}, u32[]{:S(2)}) async-start(bf16[4,12,2,8,4224]{4,3,2,1,0:T(8,128)(2,1)} %broadcast_select_fusion), calls=%async_computation.1 | async-start | bytes 12976128 | tf_op jit(solution)/shard_map/all_to_all | solution.py:97
  49.1 0.5 broadcast.226
  49.6 0.7 reduce.11
  50.4 70.5 %all-to-all-done.1 = bf16[4,12,2,8,4224]{4,3,2,1,0:T(8,128)(2,1)} async-done(((bf16[4,12,2,8,4224]{4,3,2,1,0:T(8,128)(2,1)}), bf16[4,12,2,8,4224]{4,3,2,1,0:T(8,128)(2,1)}, u32[]{:S(2)}, u32[]{:S(2)}) %all-to-all-start.1) | async-done | bytes 6488096 | tf_op jit(solution)/shard_map/all_to_all | solution.py:97
  120.9 5.0 %fusion.18 = (bf16[32,2,8,4224]{3,0,2,1:T(8,128)(2,1)S(1)}, f32[32,2,8,4224]{3,0,2,1:T(8,128)S(1)}) fusion(bf16[48,2,8,4224]{3,2,1,0:T(8,128)(2,1)} %bitcast.9, s32[48]{0:T(128)S(1)} %eq.76), kind=kOutput, calls=%fused_computation.44 | convolution fusion | flops 209782272 | bytes 19464384 | tf_op jit(solution)/shard_map/sn,sprw->nprw/dot_general | solution.py:101
  126.1 3.6 %collective-permute-start = (bf16[8,2,8,4224]{3,0,2,1:T(8,128)(2,1)S(1)}, bf16[8,2,8,4224]{3,0,2,1:T(8,128)(2,1)S(1)}, u32[]{:S(2)}, u32[]{:S(2)}) collective-permute-start(bf16[8,2,8,4224]{3,0,2,1:T(8,128)(2,1)S(1)} %get-tuple-element.56), channel_id=1, source_target_pairs={{0,1},{1,2},{2,3},{4,5},{5,6},{6,7},{8,9},{9,10},{10,11},{12,13},{... | collective-permute-start | bytes 3244040 | tf_op jit(solution)/shard_map/ppermute | solution.py:17
  129.7 1.3 collective-permute-start.1
  131.3 20.6 %collective-permute-done = bf16[8,2,8,4224]{3,0,2,1:T(8,128)(2,1)S(1)} collective-permute-done((bf16[8,2,8,4224]{3,0,2,1:T(8,128)(2,1)S(1)}, bf16[8,2,8,4224]{3,0,2,1:T(8,128)(2,1)S(1)}, u32[]{:S(2)}, u32[]{:S(2)}) %collective-permute-start) | collective-permute-done | bytes 1081376 | tf_op jit(solution)/shard_map/ppermute | solution.py:17
  152.2 3.7 %collective-permute-done.1 = bf16[8,2,8,4224]{3,0,2,1:T(8,128)(2,1)S(1)} collective-permute-done((bf16[8,2,8,4224]{3,0,2,1:T(8,128)(2,1)S(1)}, bf16[8,2,8,4224]{3,0,2,1:T(8,128)(2,1)S(1)}, u32[]{:S(2)}, u32[]{:S(2)}) %collective-permute-start.1) | collective-permute-done | bytes 1081376 | tf_op jit(solution)/shard_map/ppermute | solution.py:17
  156.5 4.4 %collective-permute-start.2 = (bf16[16,2,8,128]{3,0,2,1:T(8,128)(2,1)S(1)}, bf16[16,2,8,128]{3,0,2,1:T(8,128)(2,1)S(1)}, u32[]{:S(2)}, u32[]{:S(2)}) collective-permute-start(bf16[16,2,8,128]{3,0,2,1:T(8,128)(2,1)S(1)} %get-tuple-element.58), channel_id=1, source_target_pairs={{0,4},{4,8},{8,12},{1,5},{5,9},{9,13},{2,6},{6,10},{10,14},{3,7},{... | collective-permute-start | bytes 196616 | tf_op jit(solution)/shard_map/ppermute | solution.py:17
  161.2 1.9 %collective-permute-start.3 = (bf16[16,2,8,128]{3,0,2,1:T(8,128)(2,1)S(1)}, bf16[16,2,8,128]{3,0,2,1:T(8,128)(2,1)S(1)}, u32[]{:S(2)}, u32[]{:S(2)}) collective-permute-start(bf16[16,2,8,128]{3,0,2,1:T(8,128)(2,1)S(1)} %get-tuple-element.57), channel_id=1, source_target_pairs={{4,0},{8,4},{12,8},{5,1},{9,5},{13,9},{6,2},{10,6},{14,10},{7,3},{... | collective-permute-start | bytes 196616 | tf_op jit(solution)/shard_map/ppermute | solution.py:17
  163.2 3.6 %collective-permute-done.3 = bf16[16,2,8,128]{3,0,2,1:T(8,128)(2,1)S(1)} collective-permute-done((bf16[16,2,8,128]{3,0,2,1:T(8,128)(2,1)S(1)}, bf16[16,2,8,128]{3,0,2,1:T(8,128)(2,1)S(1)}, u32[]{:S(2)}, u32[]{:S(2)}) %collective-permute-start.3) | collective-permute-done | bytes 65568 | tf_op jit(solution)/shard_map/ppermute | solution.py:17
  167.1 1.9 %copy.37 = f32[16,1,8,3968]{3,2,0,1:T(8,128)} copy(f32[16,1,8,3968]{3,0,2,1:T(8,128)S(1)} %fusion.4) | data formatting | bytes 4063232 | tf_op jit(solution)/shard_map/div | solution.py:122
  (24 shorter events, 2.2 us)
Async XLA Ops:
  0.0 9.5 %copy-start = (f32[1,8]{1,0:T(1,128)S(1)}, f32[1,8]{1,0:T(1,128)}, u32[]{:S(2)}) copy-start(f32[1,8]{1,0:T(1,128)} %param.19) | copy-start | bytes 100
  3.3 40.4 %all-to-all-start = ((s32[4,1,12]{2,1,0:T(1,128)}), s32[4,1,12]{2,1,0:T(1,128)S(1)}, u32[]{:S(2)}, u32[]{:S(2)}) async-start(s32[4,1,12]{2,1,0:T(1,128)} %bitcast.3), calls=%async_computation | async-start | bytes 4096 | tf_op jit(solution)/shard_map/all_to_all | solution.py:98
  43.7 77.2 %all-to-all-start.1 = ((bf16[4,12,2,8,4224]{4,3,2,1,0:T(8,128)(2,1)}), bf16[4,12,2,8,4224]{4,3,2,1,0:T(8,128)(2,1)}, u32[]{:S(2)}, u32[]{:S(2)}) async-start(bf16[4,12,2,8,4224]{4,3,2,1,0:T(8,128)(2,1)} %broadcast_select_fusion), calls=%async_computation.1 | async-start | bytes 12976128 | tf_op jit(solution)/shard_map/all_to_all | solution.py:97
  126.1 25.8 %collective-permute-start = (bf16[8,2,8,4224]{3,0,2,1:T(8,128)(2,1)S(1)}, bf16[8,2,8,4224]{3,0,2,1:T(8,128)(2,1)S(1)}, u32[]{:S(2)}, u32[]{:S(2)}) collective-permute-start(bf16[8,2,8,4224]{3,0,2,1:T(8,128)(2,1)S(1)} %get-tuple-element.56), channel_id=1, source_target_pairs={{0,1},{1,2},{2,3},{4,5},{5,6},{6,7},{8,9},{9,10},{10,11},{12,13},{... | collective-permute-start | bytes 3244040 | tf_op jit(solution)/shard_map/ppermute | solution.py:17
  129.7 26.1 %collective-permute-start.1 = (bf16[8,2,8,4224]{3,0,2,1:T(8,128)(2,1)S(1)}, bf16[8,2,8,4224]{3,0,2,1:T(8,128)(2,1)S(1)}, u32[]{:S(2)}, u32[]{:S(2)}) collective-permute-start(bf16[8,2,8,4224]{3,0,2,1:T(8,128)(2,1)S(1)} %get-tuple-element.55), channel_id=1, source_target_pairs={{1,0},{2,1},{3,2},{5,4},{6,5},{7,6},{9,8},{10,9},{11,10},{13,12},{... | collective-permute-start | bytes 3244040 | tf_op jit(solution)/shard_map/ppermute | solution.py:17
  156.5 6.7 %collective-permute-start.2 = (bf16[16,2,8,128]{3,0,2,1:T(8,128)(2,1)S(1)}, bf16[16,2,8,128]{3,0,2,1:T(8,128)(2,1)S(1)}, u32[]{:S(2)}, u32[]{:S(2)}) collective-permute-start(bf16[16,2,8,128]{3,0,2,1:T(8,128)(2,1)S(1)} %get-tuple-element.58), channel_id=1, source_target_pairs={{0,4},{4,8},{8,12},{1,5},{5,9},{9,13},{2,6},{6,10},{10,14},{3,7},{... | collective-permute-start | bytes 196616 | tf_op jit(solution)/shard_map/ppermute | solution.py:17
  161.2 5.6 %collective-permute-start.3 = (bf16[16,2,8,128]{3,0,2,1:T(8,128)(2,1)S(1)}, bf16[16,2,8,128]{3,0,2,1:T(8,128)(2,1)S(1)}, u32[]{:S(2)}, u32[]{:S(2)}) collective-permute-start(bf16[16,2,8,128]{3,0,2,1:T(8,128)(2,1)S(1)} %get-tuple-element.57), channel_id=1, source_target_pairs={{4,0},{8,4},{12,8},{5,1},{9,5},{13,9},{6,2},{10,6},{14,10},{7,3},{... | collective-permute-start | bytes 196616 | tf_op jit(solution)/shard_map/ppermute | solution.py:17

commit v2 on v1

v2 whole, which is shorter than its diff:
```python
import jax
import jax.numpy as jnp
from jax import lax
from jax.experimental import pallas as pl
from jax.experimental.pallas import tpu as pltpu
from jax.sharding import PartitionSpec as P

OVY = 64
PR = 128
RB = 8
CHUNKS = 3
ROW_PIECE = 640


def shifted(value, axis, steps):
    count = lax.axis_size(axis)
    first, last = (max(0, -steps), min(count, count - steps))
    return lax.ppermute(value, axis, [(source, source + steps) for source in range(first, last)])


def make_warp_kernel(start, width, exposures):
    def kernel(w_ref, idx_ref, img_hbm, mask_hbm, rk_ref, ck_ref, out_ref, img_buf, mask_buf, rw_buf, blk_buf, sems):
        ph = rk_ref.shape[2]
        tiles, kw, tw = ck_ref.shape
        blocks = ph // RB
        copies = []
        for e in range(exposures):
            ci = pltpu.make_async_copy(img_hbm.at[0, e, :, pl.ds(start, width)], img_buf.at[e], sems.at[0, e])
            cm = pltpu.make_async_copy(mask_hbm.at[0, e, :, pl.ds(start, width)], mask_buf.at[e], sems.at[1, e])
            ci.start()
            cm.start()
            copies.append((ci, cm))
        for e in range(exposures):
            ci, cm = copies[e]
            ci.wait()
            cm.wait()
            rk = rk_ref[0, e]
            piece_start = 0
            while piece_start < width:
                piece = min(ROW_PIECE, width - piece_start)
                cols = pl.ds(piece_start, piece)
                good = mask_buf[e, :, cols] == 0
                img = img_buf[e, :, cols]
                p0 = jnp.where(good, img, jnp.zeros_like(img))
                p1 = good.astype(jnp.bfloat16)
                rw_buf[0:ph, cols] = jnp.dot(rk, p0, preferred_element_type=jnp.float32).astype(jnp.bfloat16)
                rw_buf[ph : 2 * ph, cols] = jnp.dot(rk, p1, preferred_element_type=jnp.float32).astype(jnp.bfloat16)
                piece_start += piece
            weight = w_ref[e]

            def tile(t, carry):
                off = pl.multiple_of(t * tw, tw)
                x = rw_buf[:, pl.ds(off, kw)]
                r = jnp.dot(x, ck_ref[t], preferred_element_type=jnp.float32) * weight
                rows = pl.ds(e * blocks, blocks)
                blk_buf[rows, 0, :, pl.ds(off, tw)] = r[0:ph].reshape(blocks, RB, tw).astype(jnp.bfloat16)
                blk_buf[rows, 1, :, pl.ds(off, tw)] = r[ph : 2 * ph].reshape(blocks, RB, tw).astype(jnp.bfloat16)
                return carry

            lax.fori_loop(0, tiles, tile, 0)

        def gather(slot, carry):
            out_ref[slot] = blk_buf[idx_ref[slot]]
            return carry

        lax.fori_loop(0, out_ref.shape[0], gather, 0)

    return kernel


def warp_chunk(chunk, weights, send_idx, images, masks, row_kernels, col_kernel):
    _, exposures, hin, win = images.shape
    ph = row_kernels.shape[2]
    tiles, kw, tw = col_kernel.shape
    per = tiles // CHUNKS
    width = per * tw
    window = width + kw - tw
    start = chunk * width
    blocks = ph // RB
    slots = send_idx.shape[0]
    return pl.pallas_call(
        make_warp_kernel(start, window, exposures),
        grid=(1,),
        in_specs=[
            pl.BlockSpec(memory_space=pltpu.SMEM),
            pl.BlockSpec(memory_space=pltpu.SMEM),
            pl.BlockSpec(memory_space=pl.ANY),
            pl.BlockSpec(memory_space=pl.ANY),
            pl.BlockSpec(memory_space=pltpu.VMEM),
            pl.BlockSpec((per, kw, tw), lambda i: (chunk, 0, 0)),
        ],
        out_specs=pl.BlockSpec(memory_space=pltpu.VMEM),
        out_shape=jax.ShapeDtypeStruct((slots, 2, RB, width), jnp.bfloat16),
        scratch_shapes=[
            pltpu.VMEM((exposures, hin, window), jnp.bfloat16),
            pltpu.VMEM((exposures, hin, window), jnp.int32),
            pltpu.VMEM((2 * ph, window), jnp.bfloat16),
            pltpu.VMEM((exposures * blocks, 2, RB, width), jnp.bfloat16),
            pltpu.SemaphoreType.DMA((2, exposures)),
        ],
        compiler_params=pltpu.CompilerParams(vmem_limit_bytes=48 * 1024 * 1024),
        cost_estimate=pl.CostEstimate(
            flops=exposures * (8 * ph * hin * window + 4 * ph * kw * width),
            transcendentals=0,
            bytes_accessed=exposures * hin * window * 6 + per * kw * tw * 2 + slots * 2 * RB * width * 2,
        ),
    )(weights, send_idx, images, masks, row_kernels, col_kernel)


def local(images, masks, row_kernels, col_kernel, inv_var, dest_col, dest_row):
    exposures = images.shape[1]
    tile_width = col_kernel.shape[2]
    cw = col_kernel.shape[0] * tile_width
    pw = cw - 2 * tile_width
    width = cw // CHUNKS
    first_exp = lax.axis_index("skyx") * exposures
    weights = lax.dynamic_slice_in_dim(inv_var[0], first_exp, exposures)

    slot_dest = dest_col[0, :, 0]
    slot_rows = dest_row[0]
    slot_count = slot_dest.shape[0]
    peers = lax.axis_size("skyx")
    capacity = max(2, (3 * slot_count + 2 * peers - 1) // (2 * peers))
    positions = (PR + 2 * OVY) // RB
    earlier = (jnp.arange(slot_count)[None, :] < jnp.arange(slot_count)[:, None]).astype(jnp.int32)
    onehot_dest = (slot_dest[:, None] == jnp.arange(peers)[None, :]).astype(jnp.int32)
    ranks = jnp.sum(jnp.dot(earlier, onehot_dest) * onehot_dest, axis=1)
    chosen = (slot_dest[None, None, :] == jnp.arange(peers)[:, None, None]) & (
        ranks[None, None, :] == jnp.arange(capacity)[None, :, None]
    )
    send_rows = jnp.sum(jnp.where(chosen, slot_rows[None, None, :] + 1, 0), axis=2) - 1
    send_idx = jnp.sum(jnp.where(chosen, jnp.arange(slot_count)[None, None, :] + 1, 0), axis=2) - 1
    send_idx = jnp.clip(send_idx, 0, slot_count - 1).reshape(-1)
    recv_rows = lax.all_to_all(send_rows, "skyx", split_axis=0, concat_axis=0, tiled=True)
    onehot_pos = (recv_rows.reshape(-1)[:, None] == jnp.arange(positions)[None, :]).astype(jnp.bfloat16)

    margin = OVY // RB
    inner = PR // RB
    interiors = []
    for chunk in range(CHUNKS):
        send_buf = warp_chunk(chunk, weights, send_idx, images, masks, row_kernels, col_kernel)
        send_buf = send_buf.reshape((peers, capacity) + send_buf.shape[1:])
        arrived = lax.all_to_all(send_buf, "skyx", split_axis=0, concat_axis=0, tiled=True)
        arrived = arrived.reshape((-1,) + arrived.shape[2:])
        canvas = jnp.einsum("sn,sprw->nprw", onehot_pos, arrived, preferred_element_type=jnp.float32)
        upper = canvas[:margin].astype(jnp.bfloat16)
        lower = canvas[margin + inner :].astype(jnp.bfloat16)
        from_above = shifted(lower, "skyy", 1).astype(jnp.float32)
        from_below = shifted(upper, "skyy", -1).astype(jnp.float32)
        interior = canvas[margin : margin + inner]
        interior = interior.at[:margin].add(from_above)
        interior = interior.at[inner - margin :].add(from_below)
        interiors.append(interior)

    left_part = interiors[0][..., :tile_width].astype(jnp.bfloat16)
    right_part = interiors[-1][..., width - tile_width :].astype(jnp.bfloat16)
    from_left = shifted(right_part, "skyx", 1).astype(jnp.float32)
    from_right = shifted(left_part, "skyx", -1).astype(jnp.float32)
    first = interiors[0][..., tile_width:]
    first = first.at[..., :tile_width].add(from_left)
    last = interiors[-1][..., : width - tile_width]
    last = last.at[..., width - 2 * tile_width :].add(from_right)
    core = jnp.concatenate([first] + interiors[1:-1] + [last], axis=-1)
    num = core[:, 0].reshape(PR, pw)
    den = core[:, 1].reshape(PR, pw)
    return num / jnp.maximum(den, 1.0)


def solution(mesh):
    in_specs = (
        P(("tract", "skyy"), "skyx", None, None),
        P(("tract", "skyy"), "skyx", None, None),
        P(("tract", "skyy"), "skyx", None, None),
        P("tract", None, None),
        P(("tract", "skyy"), None),
        P(("tract", "skyy"), "skyx", None),
        P(("tract", "skyy"), "skyx"),
    )
    out_specs = P(("tract", "skyy"), "skyx")
    return jax.shard_map(local, mesh=mesh, in_specs=in_specs, out_specs=out_specs, check_vma=False)
```

time: 170 us -> 136 us (0.80)
  waiting for transfers between devices: 98.4 us -> 39.1 us
  starting transfers between devices: 20.9 us -> 41.4 us
  Pallas kernels: 20.3 us -> 24.7 us
  other arithmetic: 9.83 us -> 7.06 us
  matrix products: 5.91 us -> 7.74 us
    all_to_all x1 -> x3, waiting for transfers between devices: 70.5 us -> 35.9 us  [local(): lax.all_to_all(send_buf, 'skyx', split_axis=0, concat_axis=0, tiled=True)]
    ppermute x4 -> x8, waiting for transfers between devices: 27.9 us -> 3.13 us  [shifted(): lax.ppermute(value, axis, [(source, source + steps) for source in range(f...]
    ppermute x4 -> x8, starting transfers between devices: 11.3 us -> 21.7 us  [shifted(): lax.ppermute(value, axis, [(source, source + steps) for source in range(f...]
    all_to_all x1 -> x3, starting transfers between devices: 5.35 us -> 15.4 us  [local(): lax.all_to_all(send_buf, 'skyx', split_axis=0, concat_axis=0, tiled=True)]
    gather x1 -> x0, local copies, waits for them, and re-layouts: 7.23 us -> none  [local(): jnp.take(blocks, send_idx.reshape(-1), axis=0, mode='fill', fill_value=0)]
    unnamed x4 -> x19, local copies, waits for them, and re-layouts: 2.3 us -> 8.88 us
    select_n x2 -> x0, other arithmetic: 6.18 us -> none  [local(): jnp.take(blocks, send_idx.reshape(-1), axis=0, mode='fill', fill_value=0)]
    pallas_call x1 -> x3, Pallas kernels: 20.3 us -> 24.7 us  [warp_chunk(): pl.pallas_call(make_warp_kernel(start, window, exposures), grid=(1,), in_...]
  transfers between devices with their start and end apart: 6 -> 12, of which waited for: 4 -> 5; matrix products, arithmetic and copies ran while one was open for 11% -> 12% of each run, Pallas kernels for 12% -> 18%
where the time goes in v2:
time: 136 us; the launch traced here: 135 us
  starting transfers between devices  41.4 us (30%)
  waiting for transfers between devices  39.1 us (29%)
  Pallas kernels  24.7 us (18%)
  local copies, waits for them, and re-layouts  14.3 us (11%)
  matrix products  7.74 us (6%)
  other arithmetic  7.06 us (5%)
    all_to_all x3, waiting for transfers between devices, local(): lax.all_to_all(send_buf, 'skyx', split_axis=0, concat_axis=0, tiled=True)  35.9 us
    pallas_call x3, Pallas kernels, warp_chunk(): pl.pallas_call(make_warp_kernel(start, window, exposures), grid=(1,), in_...  24.7 us
    ppermute x8, starting transfers between devices, shifted(): lax.ppermute(value, axis, [(source, source + steps) for source in range(f...  21.7 us
    all_to_all x3, starting transfers between devices, local(): lax.all_to_all(send_buf, 'skyx', split_axis=0, concat_axis=0, tiled=True)  15.4 us
    unnamed x19, local copies, waits for them, and re-layouts  8.88 us
    dot_general x3, matrix products, local(): jnp.einsum('sn,sprw->nprw', onehot_pos, arrived, preferred_element_type=j...  6.87 us
    all_to_all x1, starting transfers between devices, local(): lax.all_to_all(send_rows, 'skyx', split_axis=0, concat_axis=0, tiled=True)  4.28 us
    ppermute x8, waiting for transfers between devices, shifted(): lax.ppermute(value, axis, [(source, source + steps) for source in range(f...  3.13 us
  transfers between devices with their start and end apart: 12, of which 5 were waited for; matrix products, arithmetic and copies ran while one was open for 12% of the time, Pallas kernels for 18%

profile of v2, /device:TPU:1, one launch (start us, length us, event | category | flops | bytes accessed | tf_op | source)
XLA Modules:
  0.0 134.7 jit_solution(14591290516635842977)
XLA Ops:
  3.4 4.3 %all-to-all-start = ((s32[4,1,12]{2,1,0:T(1,128)}), s32[4,1,12]{2,1,0:T(1,128)S(1)}, u32[]{:S(2)}, u32[]{:S(2)}) async-start(s32[4,1,12]{2,1,0:T(1,128)} %bitcast.3), calls=%async_computation | async-start | bytes 4096 | tf_op jit(solution)/shard_map/all_to_all | solution.py:134
  8.9 1.7 %copy-done.1 = bf16[1,2,136,4480]{3,2,1,0:T(8,128)(2,1)S(1)} copy-done((bf16[1,2,136,4480]{3,2,1,0:T(8,128)(2,1)S(1)}, bf16[1,2,136,4480]{3,2,1,0:T(8,128)(2,1)}, u32[]{:S(2)}) %copy-start.1) | copy-done | bytes 2437144
  10.6 8.2 %shard_map.73 = bf16[48,2,8,1408]{3,2,1,0:T(8,128)(2,1)S(1)} custom-call(f32[2]{0:T(128)S(1)} %fusion.26.w_ref, s32[48]{0:T(128)S(1)} %min.12.idx_ref, bf16[1,2,136,4480]{3,2,1,0:T(8,128)(2,1)S(1)} %copy-done.1, s32[1,2,136,4480]{3,2,1,0:T(8,128)} %mask_hbm.5, bf16[1,2,128,136]{3,2,1,0:T(8,128)(2,1)S(1)} %copy.42.rk_ref, bf16[33,384,128]{2,1,0:T(8,128)(2,1)} %ck_ref.5), custom_call_target="tpu_custom_call" | custom-call | flops 1017118720 | bytes 5959680 | tf_op jit(solution)/shard_map/pallas_call | solution.py:81
  18.9 1.3 copy-done.5
  20.2 4.6 %all-to-all-start.1 = ((bf16[4,12,2,8,1408]{4,3,2,1,0:T(8,128)(2,1)}), bf16[4,12,2,8,1408]{4,3,2,1,0:T(8,128)(2,1)}, u32[]{:S(2)}, u32[]{:S(2)}) async-start(bf16[4,12,2,8,1408]{4,3,2,1,0:T(8,128)(2,1)} %bitcast.32), calls=%async_computation.1 | async-start | bytes 4325376 | tf_op jit(solution)/shard_map/all_to_all | solution.py:143
  24.8 8.3 %shard_map.74 = bf16[48,2,8,1408]{3,2,1,0:T(8,128)(2,1)S(1)} custom-call(f32[2]{0:T(128)S(1)} %fusion.26.w_ref, s32[48]{0:T(128)S(1)} %min.12.idx_ref, bf16[1,2,136,4480]{3,2,1,0:T(8,128)(2,1)S(1)} %copy-done.2, s32[1,2,136,4480]{3,2,1,0:T(8,128)} %mask_hbm.5, bf16[1,2,128,136]{3,2,1,0:T(8,128)(2,1)S(1)} %copy.42.rk_ref, bf16[33,384,128]{2,1,0:T(8,128)(2,1)} %ck_ref.5), custom_call_target="tpu_custom_call" | custom-call | flops 1017118720 | bytes 5959680 | tf_op jit(solution)/shard_map/pallas_call | solution.py:81
  33.1 1.4 %copy-done.4 = bf16[48,2,8,1408]{3,2,1,0:T(8,128)(2,1)} copy-done((bf16[48,2,8,1408]{3,2,1,0:T(8,128)(2,1)}, bf16[48,2,8,1408]{3,2,1,0:T(8,128)(2,1)S(1)}, u32[]{:S(2)}) %copy-start.4) | copy-done | bytes 2162712
  34.5 15.8 %all-to-all-done.1 = bf16[4,12,2,8,1408]{4,3,2,1,0:T(8,128)(2,1)} async-done(((bf16[4,12,2,8,1408]{4,3,2,1,0:T(8,128)(2,1)}), bf16[4,12,2,8,1408]{4,3,2,1,0:T(8,128)(2,1)}, u32[]{:S(2)}, u32[]{:S(2)}) %all-to-all-start.1) | async-done | bytes 2162720 | tf_op jit(solution)/shard_map/all_to_all | solution.py:143
  50.3 5.4 %all-to-all-start.2 = ((bf16[4,12,2,8,1408]{4,3,2,1,0:T(8,128)(2,1)}), bf16[4,12,2,8,1408]{4,3,2,1,0:T(8,128)(2,1)}, u32[]{:S(2)}, u32[]{:S(2)}) async-start(bf16[4,12,2,8,1408]{4,3,2,1,0:T(8,128)(2,1)} %bitcast.31), calls=%async_computation.2 | async-start | bytes 4325376 | tf_op jit(solution)/shard_map/all_to_all | solution.py:143
  55.7 8.2 %shard_map.75 = bf16[48,2,8,1408]{3,2,1,0:T(8,128)(2,1)S(1)} custom-call(f32[2]{0:T(128)S(1)} %fusion.26.w_ref, s32[48]{0:T(128)S(1)} %min.12.idx_ref, bf16[1,2,136,4480]{3,2,1,0:T(8,128)(2,1)S(1)} %copy-done.2, s32[1,2,136,4480]{3,2,1,0:T(8,128)} %mask_hbm.5, bf16[1,2,128,136]{3,2,1,0:T(8,128)(2,1)S(1)} %copy.42.rk_ref, bf16[33,384,128]{2,1,0:T(8,128)(2,1)} %ck_ref.5), custom_call_target="tpu_custom_call" | custom-call | flops 1017118720 | bytes 5959680 | tf_op jit(solution)/shard_map/pallas_call | solution.py:81
  63.9 1.3 copy-done.3
  66.5 14.6 %all-to-all-done.2 = bf16[4,12,2,8,1408]{4,3,2,1,0:T(8,128)(2,1)} async-done(((bf16[4,12,2,8,1408]{4,3,2,1,0:T(8,128)(2,1)}), bf16[4,12,2,8,1408]{4,3,2,1,0:T(8,128)(2,1)}, u32[]{:S(2)}, u32[]{:S(2)}) %all-to-all-start.2) | async-done | bytes 2162720 | tf_op jit(solution)/shard_map/all_to_all | solution.py:143
  81.2 5.4 %all-to-all-start.3 = ((bf16[4,12,2,8,1408]{4,3,2,1,0:T(8,128)(2,1)}), bf16[4,12,2,8,1408]{4,3,2,1,0:T(8,128)(2,1)}, u32[]{:S(2)}, u32[]{:S(2)}) async-start(bf16[4,12,2,8,1408]{4,3,2,1,0:T(8,128)(2,1)} %bitcast.30), calls=%async_computation.3 | async-start | bytes 4325376 | tf_op jit(solution)/shard_map/all_to_all | solution.py:143
  86.6 2.3 %fusion.30 = (bf16[32,2,8,1408]{3,0,2,1:T(8,128)(2,1)S(1)}, f32[32,2,8,1408]{3,0,2,1:T(8,128)S(1)}) fusion(bf16[48,2,8,1408]{3,2,1,0:T(8,128)(2,1)} %bitcast.8, s32[48]{0:T(128)S(1)} %eq.76), kind=kOutput, calls=%fused_computation.53 | convolution fusion | flops 69928448 | bytes 6488256 | tf_op jit(solution)/shard_map/sn,sprw->nprw/dot_general | solution.py:145
  90.8 4.4 %collective-permute-start = (bf16[8,2,8,1408]{3,0,2,1:T(8,128)(2,1)}, bf16[8,2,8,1408]{3,0,2,1:T(8,128)(2,1)}, u32[]{:S(2)}, u32[]{:S(2)}) collective-permute-start(bf16[8,2,8,1408]{3,0,2,1:T(8,128)(2,1)} %get-tuple-element.106), channel_id=1, source_target_pairs={{0,1},{1,2},{2,3},{4,5},{5,6},{6,7},{8,9},{9,10},{10,11},{12,13},{... | collective-permute-start | bytes 1081352 | tf_op jit(solution)/shard_map/ppermute | solution.py:18
  96.5 2.3 %fusion.31 = (bf16[32,2,8,1408]{3,0,2,1:T(8,128)(2,1)S(1)}, f32[32,2,8,1408]{3,0,2,1:T(8,128)S(1)}) fusion(bf16[48,2,8,1408]{3,2,1,0:T(8,128)(2,1)} %bitcast.11, s32[48]{0:T(128)S(1)} %eq.76), kind=kOutput, calls=%fused_computation.54 | convolution fusion | flops 69928448 | bytes 6488256 | tf_op jit(solution)/shard_map/sn,sprw->nprw/dot_general | solution.py:145
  100.6 4.7 %collective-permute-start.2 = (bf16[8,2,8,1408]{3,0,2,1:T(8,128)(2,1)}, bf16[8,2,8,1408]{3,0,2,1:T(8,128)(2,1)}, u32[]{:S(2)}, u32[]{:S(2)}) collective-permute-start(bf16[8,2,8,1408]{3,0,2,1:T(8,128)(2,1)} %get-tuple-element.108), channel_id=1, source_target_pairs={{0,1},{1,2},{2,3},{4,5},{5,6},{6,7},{8,9},{9,10},{10,11},{12,13},{... | collective-permute-start | bytes 1081352 | tf_op jit(solution)/shard_map/ppermute | solution.py:18
  106.6 5.5 %all-to-all-done.3 = bf16[4,12,2,8,1408]{4,3,2,1,0:T(8,128)(2,1)} async-done(((bf16[4,12,2,8,1408]{4,3,2,1,0:T(8,128)(2,1)}), bf16[4,12,2,8,1408]{4,3,2,1,0:T(8,128)(2,1)}, u32[]{:S(2)}, u32[]{:S(2)}) %all-to-all-start.3) | async-done | bytes 2162720 | tf_op jit(solution)/shard_map/all_to_all | solution.py:143
  112.1 2.3 %fusion.32 = (bf16[32,2,8,1408]{3,0,2,1:T(8,128)(2,1)S(1)}, f32[32,2,8,1408]{3,0,2,1:T(8,128)S(1)}) fusion(bf16[48,2,8,1408]{3,2,1,0:T(8,128)(2,1)} %bitcast.13, s32[48]{0:T(128)S(1)} %eq.76), kind=kOutput, calls=%fused_computation.55 | convolution fusion | flops 69928448 | bytes 6488256 | tf_op jit(solution)/shard_map/sn,sprw->nprw/dot_general | solution.py:145
  114.6 3.7 %collective-permute-start.5 = (bf16[8,2,8,1408]{3,0,2,1:T(8,128)(2,1)S(1)}, bf16[8,2,8,1408]{3,0,2,1:T(8,128)(2,1)S(1)}, u32[]{:S(2)}, u32[]{:S(2)}) collective-permute-start(bf16[8,2,8,1408]{3,0,2,1:T(8,128)(2,1)S(1)} %get-tuple-element.104), channel_id=1, source_target_pairs={{0,1},{1,2},{2,3},{4,5},{5,6},{6,7},{8,9},{9,10},{10,11},{12,13},{... | collective-permute-start | bytes 1081352 | tf_op jit(solution)/shard_map/ppermute | solution.py:18
  122.0 3.2 %collective-permute-start.4 = (bf16[16,2,8,128]{3,0,2,1:T(8,128)(2,1)S(1)}, bf16[16,2,8,128]{3,0,2,1:T(8,128)(2,1)S(1)}, u32[]{:S(2)}, u32[]{:S(2)}) collective-permute-start(bf16[16,2,8,128]{3,0,2,1:T(8,128)(2,1)S(1)} %slice.367), channel_id=1, source_target_pairs={{0,4},{4,8},{8,12},{1,5},{5,9},{9,13},{2,6},{6,10},{10,14},{3,7},{... | collective-permute-start | bytes 196616 | tf_op jit(solution)/shard_map/ppermute | solution.py:18
  126.6 1.9 %collective-permute-start.7 = (bf16[16,2,8,128]{3,0,2,1:T(8,128)(2,1)S(1)}, bf16[16,2,8,128]{3,0,2,1:T(8,128)(2,1)S(1)}, u32[]{:S(2)}, u32[]{:S(2)}) collective-permute-start(bf16[16,2,8,128]{3,0,2,1:T(8,128)(2,1)S(1)} %slice.366), channel_id=1, source_target_pairs={{4,0},{8,4},{12,8},{5,1},{9,5},{13,9},{6,2},{10,6},{14,10},{7,3},{... | collective-permute-start | bytes 196616 | tf_op jit(solution)/shard_map/ppermute | solution.py:18
  129.3 2.9 %collective-permute-done.7 = bf16[16,2,8,128]{3,0,2,1:T(8,128)(2,1)S(1)} collective-permute-done((bf16[16,2,8,128]{3,0,2,1:T(8,128)(2,1)S(1)}, bf16[16,2,8,128]{3,0,2,1:T(8,128)(2,1)S(1)}, u32[]{:S(2)}, u32[]{:S(2)}) %collective-permute-start.7) | collective-permute-done | bytes 65568 | tf_op jit(solution)/shard_map/ppermute | solution.py:18
  132.8 1.9 %copy.65 = f32[16,1,8,3968]{3,2,0,1:T(8,128)} copy(f32[16,1,8,3968]{3,0,2,1:T(8,128)S(1)} %fusion.6) | data formatting | bytes 4063232 | tf_op jit(solution)/shard_map/div | solution.py:166
  (58 shorter events, 18.7 us)
Async XLA Ops:
  0.0 8.9 %copy-start = (f32[1,8]{1,0:T(1,128)S(1)}, f32[1,8]{1,0:T(1,128)}, u32[]{:S(2)}) copy-start(f32[1,8]{1,0:T(1,128)} %param.27) | copy-start | bytes 100
  3.4 16.8 %all-to-all-start = ((s32[4,1,12]{2,1,0:T(1,128)}), s32[4,1,12]{2,1,0:T(1,128)S(1)}, u32[]{:S(2)}, u32[]{:S(2)}) async-start(s32[4,1,12]{2,1,0:T(1,128)} %bitcast.3), calls=%async_computation | async-start | bytes 4096 | tf_op jit(solution)/shard_map/all_to_all | solution.py:134
  8.9 1.7 %copy-start.1 = (bf16[1,2,136,4480]{3,2,1,0:T(8,128)(2,1)S(1)}, bf16[1,2,136,4480]{3,2,1,0:T(8,128)(2,1)}, u32[]{:S(2)}) copy-start(bf16[1,2,136,4480]{3,2,1,0:T(8,128)(2,1)} %img_hbm.5) | copy-start | bytes 7311364
  18.9 1.3 copy-start.5
  20.2 4.6 %copy-start.2 = (bf16[1,2,136,4480]{3,2,1,0:T(8,128)(2,1)S(1)}, bf16[1,2,136,4480]{3,2,1,0:T(8,128)(2,1)}, u32[]{:S(2)}) copy-start(bf16[1,2,136,4480]{3,2,1,0:T(8,128)(2,1)} %img_hbm.5) | copy-start | bytes 7311364
  20.2 30.1 %all-to-all-start.1 = ((bf16[4,12,2,8,1408]{4,3,2,1,0:T(8,128)(2,1)}), bf16[4,12,2,8,1408]{4,3,2,1,0:T(8,128)(2,1)}, u32[]{:S(2)}, u32[]{:S(2)}) async-start(bf16[4,12,2,8,1408]{4,3,2,1,0:T(8,128)(2,1)} %bitcast.32), calls=%async_computation.1 | async-start | bytes 4325376 | tf_op jit(solution)/shard_map/all_to_all | solution.py:143
  33.1 1.4 %copy-start.4 = (bf16[48,2,8,1408]{3,2,1,0:T(8,128)(2,1)}, bf16[48,2,8,1408]{3,2,1,0:T(8,128)(2,1)S(1)}, u32[]{:S(2)}) copy-start(bf16[48,2,8,1408]{3,2,1,0:T(8,128)(2,1)S(1)} %shard_map.74) | copy-start | bytes 6488068
  50.3 30.9 %all-to-all-start.2 = ((bf16[4,12,2,8,1408]{4,3,2,1,0:T(8,128)(2,1)}), bf16[4,12,2,8,1408]{4,3,2,1,0:T(8,128)(2,1)}, u32[]{:S(2)}, u32[]{:S(2)}) async-start(bf16[4,12,2,8,1408]{4,3,2,1,0:T(8,128)(2,1)} %bitcast.31), calls=%async_computation.2 | async-start | bytes 4325376 | tf_op jit(solution)/shard_map/all_to_all | solution.py:143
  63.9 1.3 copy-start.3
  81.2 31.0 %all-to-all-start.3 = ((bf16[4,12,2,8,1408]{4,3,2,1,0:T(8,128)(2,1)}), bf16[4,12,2,8,1408]{4,3,2,1,0:T(8,128)(2,1)}, u32[]{:S(2)}, u32[]{:S(2)}) async-start(bf16[4,12,2,8,1408]{4,3,2,1,0:T(8,128)(2,1)} %bitcast.30), calls=%async_computation.3 | async-start | bytes 4325376 | tf_op jit(solution)/shard_map/all_to_all | solution.py:143
  88.9 1.8 %copy-start.6 = (f32[32,2,8,1408]{3,0,2,1:T(8,128)}, f32[32,2,8,1408]{3,0,2,1:T(8,128)S(1)}, u32[]{:S(2)}) copy-start(f32[32,2,8,1408]{3,0,2,1:T(8,128)S(1)} %get-tuple-element.110) | copy-start | bytes 8650756
  90.8 34.4 %collective-permute-start = (bf16[8,2,8,1408]{3,0,2,1:T(8,128)(2,1)}, bf16[8,2,8,1408]{3,0,2,1:T(8,128)(2,1)}, u32[]{:S(2)}, u32[]{:S(2)}) collective-permute-start(bf16[8,2,8,1408]{3,0,2,1:T(8,128)(2,1)} %get-tuple-element.106), channel_id=1, source_target_pairs={{0,1},{1,2},{2,3},{4,5},{5,6},{6,7},{8,9},{9,10},{10,11},{12,13},{... | collective-permute-start | bytes 1081352 | tf_op jit(solution)/shard_map/ppermute | solution.py:18
  95.2 31.3 %collective-permute-start.1 = (bf16[8,2,8,1408]{3,0,2,1:T(8,128)(2,1)}, bf16[8,2,8,1408]{3,0,2,1:T(8,128)(2,1)S(1)}, u32[]{:S(2)}, u32[]{:S(2)}) collective-permute-start(bf16[8,2,8,1408]{3,0,2,1:T(8,128)(2,1)} %get-tuple-element.105), channel_id=1, source_target_pairs={{1,0},{2,1},{3,2},{5,4},{6,5},{7,6},{9,8},{10,9},{11,10},{13,12},{... | collective-permute-start | bytes 1081352 | tf_op jit(solution)/shard_map/ppermute | solution.py:18
  98.8 1.9 %copy-start.7 = (f32[32,2,8,1408]{3,0,2,1:T(8,128)}, f32[32,2,8,1408]{3,0,2,1:T(8,128)S(1)}, u32[]{:S(2)}) copy-start(f32[32,2,8,1408]{3,0,2,1:T(8,128)S(1)} %get-tuple-element.112) | copy-start | bytes 8650756
  100.6 17.7 %collective-permute-start.2 = (bf16[8,2,8,1408]{3,0,2,1:T(8,128)(2,1)}, bf16[8,2,8,1408]{3,0,2,1:T(8,128)(2,1)}, u32[]{:S(2)}, u32[]{:S(2)}) collective-permute-start(bf16[8,2,8,1408]{3,0,2,1:T(8,128)(2,1)} %get-tuple-element.108), channel_id=1, source_target_pairs={{0,1},{1,2},{2,3},{4,5},{5,6},{6,7},{8,9},{9,10},{10,11},{12,13},{... | collective-permute-start | bytes 1081352 | tf_op jit(solution)/shard_map/ppermute | solution.py:18
  105.3 15.5 %collective-permute-start.3 = (bf16[8,2,8,1408]{3,0,2,1:T(8,128)(2,1)}, bf16[8,2,8,1408]{3,0,2,1:T(8,128)(2,1)}, u32[]{:S(2)}, u32[]{:S(2)}) collective-permute-start(bf16[8,2,8,1408]{3,0,2,1:T(8,128)(2,1)} %get-tuple-element.107), channel_id=1, source_target_pairs={{1,0},{2,1},{3,2},{5,4},{6,5},{7,6},{9,8},{10,9},{11,10},{13,12},{... | collective-permute-start | bytes 1081352 | tf_op jit(solution)/shard_map/ppermute | solution.py:18
  114.6 13.9 %collective-permute-start.5 = (bf16[8,2,8,1408]{3,0,2,1:T(8,128)(2,1)S(1)}, bf16[8,2,8,1408]{3,0,2,1:T(8,128)(2,1)S(1)}, u32[]{:S(2)}, u32[]{:S(2)}) collective-permute-start(bf16[8,2,8,1408]{3,0,2,1:T(8,128)(2,1)S(1)} %get-tuple-element.104), channel_id=1, source_target_pairs={{0,1},{1,2},{2,3},{4,5},{5,6},{6,7},{8,9},{9,10},{10,11},{12,13},{... | collective-permute-start | bytes 1081352 | tf_op jit(solution)/shard_map/ppermute | solution.py:18
  118.3 10.6 %collective-permute-start.6 = (bf16[8,2,8,1408]{3,0,2,1:T(8,128)(2,1)S(1)}, bf16[8,2,8,1408]{3,0,2,1:T(8,128)(2,1)S(1)}, u32[]{:S(2)}, u32[]{:S(2)}) collective-permute-start(bf16[8,2,8,1408]{3,0,2,1:T(8,128)(2,1)S(1)} %get-tuple-element.103), channel_id=1, source_target_pairs={{1,0},{2,1},{3,2},{5,4},{6,5},{7,6},{9,8},{10,9},{11,10},{13,12},{... | collective-permute-start | bytes 1081352 | tf_op jit(solution)/shard_map/ppermute | solution.py:18
  122.0 7.3 %collective-permute-start.4 = (bf16[16,2,8,128]{3,0,2,1:T(8,128)(2,1)S(1)}, bf16[16,2,8,128]{3,0,2,1:T(8,128)(2,1)S(1)}, u32[]{:S(2)}, u32[]{:S(2)}) collective-permute-start(bf16[16,2,8,128]{3,0,2,1:T(8,128)(2,1)S(1)} %slice.367), channel_id=1, source_target_pairs={{0,4},{4,8},{8,12},{1,5},{5,9},{9,13},{2,6},{6,10},{10,14},{3,7},{... | collective-permute-start | bytes 196616 | tf_op jit(solution)/shard_map/ppermute | solution.py:18
  126.6 5.6 %collective-permute-start.7 = (bf16[16,2,8,128]{3,0,2,1:T(8,128)(2,1)S(1)}, bf16[16,2,8,128]{3,0,2,1:T(8,128)(2,1)S(1)}, u32[]{:S(2)}, u32[]{:S(2)}) collective-permute-start(bf16[16,2,8,128]{3,0,2,1:T(8,128)(2,1)S(1)} %slice.366), channel_id=1, source_target_pairs={{4,0},{8,4},{12,8},{5,1},{9,5},{13,9},{6,2},{10,6},{14,10},{7,3},{... | collective-permute-start | bytes 196616 | tf_op jit(solution)/shard_map/ppermute | solution.py:18

commit v3 on v2

--- a/solution.py
+++ b/solution.py
@@ -107,6 +107,47 @@
     )(weights, send_idx, images, masks, row_kernels, col_kernel)
 
 
+def make_place_kernel(groups, capacity, positions, margin, inner):
+    def kernel(rows_ref, *refs):
+        recv_refs = refs[:groups]
+        upper_ref, lower_ref, int_ref, canvas = refs[groups:]
+        canvas[...] = jnp.zeros(canvas.shape, jnp.float32)
+        for g in range(groups):
+            def body(c, carry, g=g):
+                pos = rows_ref[g * capacity + c]
+
+                @pl.when((pos >= 0) & (pos < positions))
+                def _():
+                    canvas[pos] += recv_refs[g][c].astype(jnp.float32)
+
+                return carry
+
+            lax.fori_loop(0, capacity, body, 0)
+        upper_ref[...] = canvas[0:margin].astype(jnp.bfloat16)
+        lower_ref[...] = canvas[margin + inner :].astype(jnp.bfloat16)
+        int_ref[...] = canvas[margin : margin + inner]
+
+    return kernel
+
+
+def place(rows, recvs, positions, margin, inner):
+    groups = len(recvs)
+    capacity = recvs[0].shape[0]
+    block = recvs[0].shape[1:]
+    return pl.pallas_call(
+        make_place_kernel(groups, capacity, positions, margin, inner),
+        in_specs=[pl.BlockSpec(memory_space=pltpu.SMEM)] + [pl.BlockSpec(memory_space=pltpu.VMEM)] * groups,
+        out_specs=[pl.BlockSpec(memory_space=pltpu.VMEM)] * 3,
+        out_shape=[
+            jax.ShapeDtypeStruct((margin,) + block, jnp.bfloat16),
+            jax.ShapeDtypeStruct((margin,) + block, jnp.bfloat16),
+            jax.ShapeDtypeStruct((inner,) + block, jnp.float32),
+        ],
+        scratch_shapes=[pltpu.VMEM((positions,) + block, jnp.float32)],
+        compiler_params=pltpu.CompilerParams(vmem_limit_bytes=32 * 1024 * 1024),
+    )(rows, *recvs)
+
+
 def local(images, masks, row_kernels, col_kernel, inv_var, dest_col, dest_row):
     exposures = images.shape[1]
     tile_width = col_kernel.shape[2]
@@ -122,17 +163,19 @@
     peers = lax.axis_size("skyx")
     capacity = max(2, (3 * slot_count + 2 * peers - 1) // (2 * peers))
     positions = (PR + 2 * OVY) // RB
+    offsets = (slot_dest - lax.axis_index("skyx")) % peers
     earlier = (jnp.arange(slot_count)[None, :] < jnp.arange(slot_count)[:, None]).astype(jnp.int32)
-    onehot_dest = (slot_dest[:, None] == jnp.arange(peers)[None, :]).astype(jnp.int32)
+    onehot_dest = (offsets[:, None] == jnp.arange(peers)[None, :]).astype(jnp.int32)
     ranks = jnp.sum(jnp.dot(earlier, onehot_dest) * onehot_dest, axis=1)
-    chosen = (slot_dest[None, None, :] == jnp.arange(peers)[:, None, None]) & (
+    chosen = (offsets[None, None, :] == jnp.arange(peers)[:, None, None]) & (
         ranks[None, None, :] == jnp.arange(capacity)[None, :, None]
     )
     send_rows = jnp.sum(jnp.where(chosen, slot_rows[None, None, :] + 1, 0), axis=2) - 1
     send_idx = jnp.sum(jnp.where(chosen, jnp.arange(slot_count)[None, None, :] + 1, 0), axis=2) - 1
     send_idx = jnp.clip(send_idx, 0, slot_count - 1).reshape(-1)
-    recv_rows = lax.all_to_all(send_rows, "skyx", split_axis=0, concat_axis=0, tiled=True)
-    onehot_pos = (recv_rows.reshape(-1)[:, None] == jnp.arange(positions)[None, :]).astype(jnp.bfloat16)
+    rings = [[(i, (i + step) % peers) for i in range(peers)] for step in range(peers)]
+    recv_rows = [send_rows[0]] + [lax.ppermute(send_rows[step], "skyx", rings[step]) for step in range(1, peers)]
+    recv_rows = jnp.concatenate(recv_rows)
 
     margin = OVY // RB
     inner = PR // RB
@@ -140,14 +183,10 @@
     for chunk in range(CHUNKS):
         send_buf = warp_chunk(chunk, weights, send_idx, images, masks, row_kernels, col_kernel)
         send_buf = send_buf.reshape((peers, capacity) + send_buf.shape[1:])
-        arrived = lax.all_to_all(send_buf, "skyx", split_axis=0, concat_axis=0, tiled=True)
-        arrived = arrived.reshape((-1,) + arrived.shape[2:])
-        canvas = jnp.einsum("sn,sprw->nprw", onehot_pos, arrived, preferred_element_type=jnp.float32)
-        upper = canvas[:margin].astype(jnp.bfloat16)
-        lower = canvas[margin + inner :].astype(jnp.bfloat16)
+        recvs = [send_buf[0]] + [lax.ppermute(send_buf[step], "skyx", rings[step]) for step in range(1, peers)]
+        upper, lower, interior = place(recv_rows, recvs, positions, margin, inner)
         from_above = shifted(lower, "skyy", 1).astype(jnp.float32)
         from_below = shifted(upper, "skyy", -1).astype(jnp.float32)
-        interior = canvas[margin : margin + inner]
         interior = interior.at[:margin].add(from_above)
         interior = interior.at[inner - margin :].add(from_below)
         interiors.append(interior)

time: 136 us -> 116 us (0.85)
  local copies, waits for them, and re-layouts: 14.3 us -> 3.93 us
  matrix products: 7.74 us -> 0.14 us
  Pallas kernels: 24.7 us -> 30.4 us
  waiting for transfers between devices: 39.1 us -> 36.4 us
  other arithmetic: 7.06 us -> 4.53 us
  starting transfers between devices: 41.4 us -> 39.3 us
    all_to_all x4 -> x0, waiting for transfers between devices: 35.9 us -> none  [the longest x3 35.9 us: local(): lax.all_to_all(send_buf, 'skyx', split_axis=0, concat_axis=0, tiled=True)]
    ppermute x0 -> x12, waiting for transfers between devices: none -> 28.6 us  [the longest x9 28.5 us: local(): lax.ppermute(send_buf[step], 'skyx', rings[step])]
    ppermute x0 -> x12, starting transfers between devices: none -> 19.8 us  [the longest x9 16.7 us: local(): lax.ppermute(send_buf[step], 'skyx', rings[step])]
    all_to_all x4 -> x0, starting transfers between devices: 19.7 us -> none  [the longest x3 15.4 us: local(): lax.all_to_all(send_buf, 'skyx', split_axis=0, concat_axis=0, tiled=True)]
    dot_general x3 -> x0, matrix products: 6.87 us -> none  [local(): jnp.einsum('sn,sprw->nprw', onehot_pos, arrived, preferred_element_type=j...]
    unnamed x19 -> x5, local copies, waits for them, and re-layouts: 8.88 us -> 2.7 us
    pallas_call x0 -> x3, Pallas kernels: none -> 5.57 us  [place(): pl.pallas_call(make_place_kernel(groups, capacity, positions, margin, inn...]
    ppermute x8, waiting for transfers between devices: 3.13 us -> 7.83 us  [shifted(): lax.ppermute(value, axis, [(source, source + steps) for source in range(f...]
  transfers between devices with their start and end apart: 12 -> 20, of which waited for: 5 -> 6; matrix products, arithmetic and copies ran while one was open for 12% -> 2% of each run, Pallas kernels for 18% -> 26%
where the time goes in v3:
time: 116 us; the launch traced here: 115 us
  starting transfers between devices  39.3 us (34%)
  waiting for transfers between devices  36.4 us (31%)
  Pallas kernels  30.4 us (26%)
  other arithmetic  4.53 us (4%)
  local copies, waits for them, and re-layouts  3.93 us (3%)
    ppermute x9, waiting for transfers between devices, local(): lax.ppermute(send_buf[step], 'skyx', rings[step])  28.5 us
    pallas_call x3, Pallas kernels, warp_chunk(): pl.pallas_call(make_warp_kernel(start, window, exposures), grid=(1,), in_...  24.8 us
    ppermute x8, starting transfers between devices, shifted(): lax.ppermute(value, axis, [(source, source + steps) for source in range(f...  19.5 us
    ppermute x9, starting transfers between devices, local(): lax.ppermute(send_buf[step], 'skyx', rings[step])  16.7 us
    ppermute x8, waiting for transfers between devices, shifted(): lax.ppermute(value, axis, [(source, source + steps) for source in range(f...  7.83 us
    pallas_call x3, Pallas kernels, place(): pl.pallas_call(make_place_kernel(groups, capacity, positions, margin, inn...  5.57 us
    ppermute x3, starting transfers between devices, local(): lax.ppermute(send_rows[step], 'skyx', rings[step])  3.14 us
    unnamed x5, local copies, waits for them, and re-layouts  2.7 us
  transfers between devices with their start and end apart: 20, of which 6 were waited for; matrix products, arithmetic and copies ran while one was open for 2% of the time, Pallas kernels for 26%

profile of v3, /device:TPU:1, one launch (start us, length us, event | category | flops | bytes accessed | tf_op | source)
XLA Modules:
  0.0 115.1 jit_solution(15274399005031504328)
XLA Ops:
  2.2 2.7 %collective-permute-start = (s32[12]{0:T(128)S(1)}, s32[12]{0:T(128)S(1)}, u32[]{:S(2)}, u32[]{:S(2)}) collective-permute-start(s32[12]{0:T(128)S(1)} %get-tuple-element.122), channel_id=1, source_target_pairs={{0,4},{4,8},{8,12},{12,0},{1,5},{5,9},{9,13},{13,1},{2,6},{6,10},{... | collective-permute-start | bytes 152 | tf_op jit(solution)/shard_map/ppermute | solution.py:177
  6.7 1.7 %copy-done.1 = bf16[1,2,136,4480]{3,2,1,0:T(8,128)(2,1)S(1)} copy-done((bf16[1,2,136,4480]{3,2,1,0:T(8,128)(2,1)S(1)}, bf16[1,2,136,4480]{3,2,1,0:T(8,128)(2,1)}, u32[]{:S(2)}) %copy-start.1) | copy-done | bytes 2437144
  8.3 8.3 %shard_map.73 = bf16[48,2,8,1408]{3,2,1,0:T(8,128)(2,1)S(1)} custom-call(f32[2]{0:T(128)S(1)} %fusion.12.w_ref, s32[48]{0:T(128)S(1)} %min.12.idx_ref, bf16[1,2,136,4480]{3,2,1,0:T(8,128)(2,1)S(1)} %copy-done.1, s32[1,2,136,4480]{3,2,1,0:T(8,128)} %mask_hbm.5, bf16[1,2,128,136]{3,2,1,0:T(8,128)(2,1)S(1)} %copy.16.rk_ref, bf16[33,384,128]{2,1,0:T(8,128)(2,1)} %ck_ref.5), custom_call_target="tpu_custom_call" | custom-call | flops 1017118720 | bytes 5959680 | tf_op jit(solution)/shard_map/pallas_call | solution.py:81
  16.8 1.3 %collective-permute-start.3 = (bf16[12,2,8,1408]{3,2,1,0:T(8,128)(2,1)S(1)}, bf16[12,2,8,1408]{3,2,1,0:T(8,128)(2,1)S(1)}, u32[]{:S(2)}, u32[]{:S(2)}) collective-permute-start(bf16[12,2,8,1408]{3,2,1,0:T(8,128)(2,1)S(1)} %get-tuple-element.131), channel_id=1, source_target_pairs={{0,4},{4,8},{8,12},{12,0},{1,5},{5,9},{9,13},{13,1},{2,6},{6,10},{... | collective-permute-start | bytes 1622024 | tf_op jit(solution)/shard_map/ppermute | solution.py:186
  18.1 1.5 %collective-permute-start.4 = (bf16[12,2,8,1408]{3,2,1,0:T(8,128)(2,1)S(1)}, bf16[12,2,8,1408]{3,2,1,0:T(8,128)(2,1)S(1)}, u32[]{:S(2)}, u32[]{:S(2)}) collective-permute-start(bf16[12,2,8,1408]{3,2,1,0:T(8,128)(2,1)S(1)} %get-tuple-element.130), channel_id=1, source_target_pairs={{0,8},{4,12},{8,0},{12,4},{1,9},{5,13},{9,1},{13,5},{2,10},{6,14},... | collective-permute-start | bytes 1622024 | tf_op jit(solution)/shard_map/ppermute | solution.py:186
  19.6 8.3 %shard_map.75 = bf16[48,2,8,1408]{3,2,1,0:T(8,128)(2,1)S(1)} custom-call(f32[2]{0:T(128)S(1)} %fusion.12.w_ref, s32[48]{0:T(128)S(1)} %min.12.idx_ref, bf16[1,2,136,4480]{3,2,1,0:T(8,128)(2,1)S(1)} %copy-done.1, s32[1,2,136,4480]{3,2,1,0:T(8,128)} %mask_hbm.5, bf16[1,2,128,136]{3,2,1,0:T(8,128)(2,1)S(1)} %copy.16.rk_ref, bf16[33,384,128]{2,1,0:T(8,128)(2,1)} %ck_ref.5), custom_call_target="tpu_custom_call" | custom-call | flops 1017118720 | bytes 5959680 | tf_op jit(solution)/shard_map/pallas_call | solution.py:81
  27.9 8.3 %shard_map.77 = bf16[48,2,8,1408]{3,2,1,0:T(8,128)(2,1)S(1)} custom-call(f32[2]{0:T(128)S(1)} %fusion.12.w_ref, s32[48]{0:T(128)S(1)} %min.12.idx_ref, bf16[1,2,136,4480]{3,2,1,0:T(8,128)(2,1)S(1)} %copy-done.1, s32[1,2,136,4480]{3,2,1,0:T(8,128)} %mask_hbm.5, bf16[1,2,128,136]{3,2,1,0:T(8,128)(2,1)S(1)} %copy.16.rk_ref, bf16[33,384,128]{2,1,0:T(8,128)(2,1)} %ck_ref.5), custom_call_target="tpu_custom_call" | custom-call | flops 1017118720 | bytes 5959680 | tf_op jit(solution)/shard_map/pallas_call | solution.py:81
  36.8 1.4 %collective-permute-start.8 = (bf16[12,2,8,1408]{3,2,1,0:T(8,128)(2,1)S(1)}, bf16[12,2,8,1408]{3,2,1,0:T(8,128)(2,1)S(1)}, u32[]{:S(2)}, u32[]{:S(2)}) collective-permute-start(bf16[12,2,8,1408]{3,2,1,0:T(8,128)(2,1)S(1)} %get-tuple-element.135), channel_id=1, source_target_pairs={{0,4},{4,8},{8,12},{12,0},{1,5},{5,9},{9,13},{13,1},{2,6},{6,10},{... | collective-permute-start | bytes 1622024 | tf_op jit(solution)/shard_map/ppermute | solution.py:186
  38.8 23.6 %collective-permute-done.10.refs_3_ = bf16[12,2,8,1408]{3,2,1,0:T(8,128)(2,1)S(1)} collective-permute-done((bf16[12,2,8,1408]{3,2,1,0:T(8,128)(2,1)S(1)}, bf16[12,2,8,1408]{3,2,1,0:T(8,128)(2,1)S(1)}, u32[]{:S(2)}, u32[]{:S(2)}) %collective-permute-start.10) | collective-permute-done | bytes 540704 | tf_op jit(solution)/shard_map/ppermute | solution.py:186
  63.0 11.6 %collective-permute-start.16 = (bf16[12,2,8,1408]{3,2,1,0:T(8,128)(2,1)S(1)}, bf16[12,2,8,1408]{3,2,1,0:T(8,128)(2,1)S(1)}, u32[]{:S(2)}, u32[]{:S(2)}) collective-permute-start(bf16[12,2,8,1408]{3,2,1,0:T(8,128)(2,1)S(1)} %get-tuple-element.125), channel_id=1, source_target_pairs={{0,12},{4,0},{8,4},{12,8},{1,13},{5,1},{9,5},{13,9},{2,14},{6,2},{... | collective-permute-start | bytes 1622024 | tf_op jit(solution)/shard_map/ppermute | solution.py:186
  74.7 1.9 %shard_map.76 = (bf16[8,2,8,1408]{3,2,1,0:T(8,128)(2,1)S(1)}, bf16[8,2,8,1408]{3,2,1,0:T(8,128)(2,1)S(1)}, f32[16,2,8,1408]{3,2,1,0:T(8,128)S(1)}) custom-call(s32[48]{0:T(128)S(1)} %pad_add_fusion.rows_ref, bf16[12,2,8,1408]{3,2,1,0:T(8,128)(2,1)S(1)} %get-tuple-element.136.refs_0_, bf16[12,2,8,1408]{3,2,1,0:T(8,128)(2,1)S(1)} %collective-permute-done.8.refs_1_, ...), custom_call_target="tpu_custom_call" | custom-call | tf_op jit(solution)/shard_map/pallas_call | solution.py:137
  76.6 3.2 %collective-permute-start.11 = (bf16[8,2,8,1408]{3,2,1,0:T(8,128)(2,1)S(1)}, bf16[8,2,8,1408]{3,2,1,0:T(8,128)(2,1)S(1)}, u32[]{:S(2)}, u32[]{:S(2)}) collective-permute-start(bf16[8,2,8,1408]{3,2,1,0:T(8,128)(2,1)S(1)} %get-tuple-element.114), channel_id=1, source_target_pairs={{0,1},{1,2},{2,3},{4,5},{5,6},{6,7},{8,9},{9,10},{10,11},{12,13},{... | collective-permute-start | bytes 1081352 | tf_op jit(solution)/shard_map/ppermute | solution.py:18
  79.8 1.9 %shard_map.74 = (bf16[8,2,8,1408]{3,2,1,0:T(8,128)(2,1)S(1)}, bf16[8,2,8,1408]{3,2,1,0:T(8,128)(2,1)S(1)}, f32[16,2,8,1408]{3,2,1,0:T(8,128)S(1)}) custom-call(s32[48]{0:T(128)S(1)} %pad_add_fusion.rows_ref, bf16[12,2,8,1408]{3,2,1,0:T(8,128)(2,1)S(1)} %get-tuple-element.132.refs_0_, bf16[12,2,8,1408]{3,2,1,0:T(8,128)(2,1)S(1)} %collective-permute-done.3.refs_1_, ...), custom_call_target="tpu_custom_call" | custom-call | tf_op jit(solution)/shard_map/pallas_call | solution.py:137
  81.7 3.2 %collective-permute-start.6 = (bf16[8,2,8,1408]{3,2,1,0:T(8,128)(2,1)S(1)}, bf16[8,2,8,1408]{3,2,1,0:T(8,128)(2,1)S(1)}, u32[]{:S(2)}, u32[]{:S(2)}) collective-permute-start(bf16[8,2,8,1408]{3,2,1,0:T(8,128)(2,1)S(1)} %get-tuple-element.111), channel_id=1, source_target_pairs={{0,1},{1,2},{2,3},{4,5},{5,6},{6,7},{8,9},{9,10},{10,11},{12,13},{... | collective-permute-start | bytes 1081352 | tf_op jit(solution)/shard_map/ppermute | solution.py:18
  84.9 1.3 %collective-permute-start.7 = (bf16[8,2,8,1408]{3,2,1,0:T(8,128)(2,1)S(1)}, bf16[8,2,8,1408]{3,2,1,0:T(8,128)(2,1)S(1)}, u32[]{:S(2)}, u32[]{:S(2)}) collective-permute-start(bf16[8,2,8,1408]{3,2,1,0:T(8,128)(2,1)S(1)} %get-tuple-element.112), channel_id=1, source_target_pairs={{1,0},{2,1},{3,2},{5,4},{6,5},{7,6},{9,8},{10,9},{11,10},{13,12},{... | collective-permute-start | bytes 1081352 | tf_op jit(solution)/shard_map/ppermute | solution.py:18
  86.2 1.3 %collective-permute-start.12 = (bf16[8,2,8,1408]{3,2,1,0:T(8,128)(2,1)S(1)}, bf16[8,2,8,1408]{3,2,1,0:T(8,128)(2,1)S(1)}, u32[]{:S(2)}, u32[]{:S(2)}) collective-permute-start(bf16[8,2,8,1408]{3,2,1,0:T(8,128)(2,1)S(1)} %get-tuple-element.115), channel_id=1, source_target_pairs={{1,0},{2,1},{3,2},{5,4},{6,5},{7,6},{9,8},{10,9},{11,10},{13,12},{... | collective-permute-start | bytes 1081352 | tf_op jit(solution)/shard_map/ppermute | solution.py:18
  87.5 4.3 %collective-permute-done.16.refs_3_ = bf16[12,2,8,1408]{3,2,1,0:T(8,128)(2,1)S(1)} collective-permute-done((bf16[12,2,8,1408]{3,2,1,0:T(8,128)(2,1)S(1)}, bf16[12,2,8,1408]{3,2,1,0:T(8,128)(2,1)S(1)}, u32[]{:S(2)}, u32[]{:S(2)}) %collective-permute-start.16) | collective-permute-done | bytes 540704 | tf_op jit(solution)/shard_map/ppermute | solution.py:186
  91.8 1.9 %shard_map.78 = (bf16[8,2,8,1408]{3,2,1,0:T(8,128)(2,1)S(1)}, bf16[8,2,8,1408]{3,2,1,0:T(8,128)(2,1)S(1)}, f32[16,2,8,1408]{3,2,1,0:T(8,128)S(1)}) custom-call(s32[48]{0:T(128)S(1)} %pad_add_fusion.rows_ref, bf16[12,2,8,1408]{3,2,1,0:T(8,128)(2,1)S(1)} %get-tuple-element.128.refs_0_, bf16[12,2,8,1408]{3,2,1,0:T(8,128)(2,1)S(1)} %collective-permute-done.14.refs_1_, ...), custom_call_target="tpu_custom_call" | custom-call | tf_op jit(solution)/shard_map/pallas_call | solution.py:137
  93.6 3.2 %collective-permute-start.17 = (bf16[8,2,8,1408]{3,2,1,0:T(8,128)(2,1)S(1)}, bf16[8,2,8,1408]{3,2,1,0:T(8,128)(2,1)S(1)}, u32[]{:S(2)}, u32[]{:S(2)}) collective-permute-start(bf16[8,2,8,1408]{3,2,1,0:T(8,128)(2,1)S(1)} %get-tuple-element.117), channel_id=1, source_target_pairs={{0,1},{1,2},{2,3},{4,5},{5,6},{6,7},{8,9},{9,10},{10,11},{12,13},{... | collective-permute-start | bytes 1081352 | tf_op jit(solution)/shard_map/ppermute | solution.py:18
  98.3 5.4 %collective-permute-done.12 = bf16[8,2,8,1408]{3,2,1,0:T(8,128)(2,1)S(1)} collective-permute-done((bf16[8,2,8,1408]{3,2,1,0:T(8,128)(2,1)S(1)}, bf16[8,2,8,1408]{3,2,1,0:T(8,128)(2,1)S(1)}, u32[]{:S(2)}, u32[]{:S(2)}) %collective-permute-start.12) | collective-permute-done | bytes 360480 | tf_op jit(solution)/shard_map/ppermute | solution.py:18
  103.9 3.4 %collective-permute-start.13 = (bf16[16,2,8,128]{3,2,1,0:T(8,128)(2,1)S(1)}, bf16[16,2,8,128]{3,2,1,0:T(8,128)(2,1)S(1)}, u32[]{:S(2)}, u32[]{:S(2)}) collective-permute-start(bf16[16,2,8,128]{3,2,1,0:T(8,128)(2,1)S(1)} %slice.402), channel_id=1, source_target_pairs={{0,4},{4,8},{8,12},{1,5},{5,9},{9,13},{2,6},{6,10},{10,14},{3,7},{... | collective-permute-start | bytes 196616 | tf_op jit(solution)/shard_map/ppermute | solution.py:18
  107.6 2.6 %collective-permute-start.19 = (bf16[16,2,8,128]{3,2,1,0:T(8,128)(2,1)S(1)}, bf16[16,2,8,128]{3,2,1,0:T(8,128)(2,1)S(1)}, u32[]{:S(2)}, u32[]{:S(2)}) collective-permute-start(bf16[16,2,8,128]{3,2,1,0:T(8,128)(2,1)S(1)} %slice.401), channel_id=1, source_target_pairs={{4,0},{8,4},{12,8},{5,1},{9,5},{13,9},{6,2},{10,6},{14,10},{7,3},{... | collective-permute-start | bytes 196616 | tf_op jit(solution)/shard_map/ppermute | solution.py:18
  111.9 1.3 %collective-permute-done.19 = bf16[16,2,8,128]{3,2,1,0:T(8,128)(2,1)S(1)} collective-permute-done((bf16[16,2,8,128]{3,2,1,0:T(8,128)(2,1)S(1)}, bf16[16,2,8,128]{3,2,1,0:T(8,128)(2,1)S(1)}, u32[]{:S(2)}, u32[]{:S(2)}) %collective-permute-start.19) | collective-permute-done | bytes 65568 | tf_op jit(solution)/shard_map/ppermute | solution.py:18
  113.5 1.6 %fusion.1 = f32[128,3968]{1,0:T(8,128)} fusion(f32[16,2,8,3968]{3,2,1,0:T(8,128)S(1)} %pad_maximum_fusion), kind=kLoop, calls=%fused_computation.3 | loop fusion | flops 1015808 | bytes 6094848 | tf_op jit(solution)/shard_map/div | solution.py:205
  (57 shorter events, 9.8 us)
Async XLA Ops:
  0.0 6.6 %copy-start = (f32[1,8]{1,0:T(1,128)S(1)}, f32[1,8]{1,0:T(1,128)}, u32[]{:S(2)}) copy-start(f32[1,8]{1,0:T(1,128)} %param.27) | copy-start | bytes 100
  2.2 34.1 %collective-permute-start = (s32[12]{0:T(128)S(1)}, s32[12]{0:T(128)S(1)}, u32[]{:S(2)}, u32[]{:S(2)}) collective-permute-start(s32[12]{0:T(128)S(1)} %get-tuple-element.122), channel_id=1, source_target_pairs={{0,4},{4,8},{8,12},{12,0},{1,5},{5,9},{9,13},{13,1},{2,6},{6,10},{... | collective-permute-start | bytes 152 | tf_op jit(solution)/shard_map/ppermute | solution.py:177
  4.9 31.5 %collective-permute-start.1 = (s32[12]{0:T(128)S(1)}, s32[12]{0:T(128)S(1)}, u32[]{:S(2)}, u32[]{:S(2)}) collective-permute-start(s32[12]{0:T(128)S(1)} %get-tuple-element.121), channel_id=1, source_target_pairs={{0,8},{4,12},{8,0},{12,4},{1,9},{5,13},{9,1},{13,5},{2,10},{6,14},... | collective-permute-start | bytes 152 | tf_op jit(solution)/shard_map/ppermute | solution.py:177
  4.9 31.9 %collective-permute-start.2 = (s32[12]{0:T(128)S(1)}, s32[12]{0:T(128)S(1)}, u32[]{:S(2)}, u32[]{:S(2)}) collective-permute-start(s32[12]{0:T(128)S(1)} %get-tuple-element.120), channel_id=1, source_target_pairs={{0,12},{4,0},{8,4},{12,8},{1,13},{5,1},{9,5},{13,9},{2,14},{6,2},{... | collective-permute-start | bytes 152 | tf_op jit(solution)/shard_map/ppermute | solution.py:177
  6.7 1.7 %copy-start.1 = (bf16[1,2,136,4480]{3,2,1,0:T(8,128)(2,1)S(1)}, bf16[1,2,136,4480]{3,2,1,0:T(8,128)(2,1)}, u32[]{:S(2)}) copy-start(bf16[1,2,136,4480]{3,2,1,0:T(8,128)(2,1)} %img_hbm.5) | copy-start | bytes 7311364
  16.8 21.4 %collective-permute-start.3 = (bf16[12,2,8,1408]{3,2,1,0:T(8,128)(2,1)S(1)}, bf16[12,2,8,1408]{3,2,1,0:T(8,128)(2,1)S(1)}, u32[]{:S(2)}, u32[]{:S(2)}) collective-permute-start(bf16[12,2,8,1408]{3,2,1,0:T(8,128)(2,1)S(1)} %get-tuple-element.131), channel_id=1, source_target_pairs={{0,4},{4,8},{8,12},{12,0},{1,5},{5,9},{9,13},{13,1},{2,6},{6,10},{... | collective-permute-start | bytes 1622024 | tf_op jit(solution)/shard_map/ppermute | solution.py:186
  18.1 58.4 %collective-permute-start.4 = (bf16[12,2,8,1408]{3,2,1,0:T(8,128)(2,1)S(1)}, bf16[12,2,8,1408]{3,2,1,0:T(8,128)(2,1)S(1)}, u32[]{:S(2)}, u32[]{:S(2)}) collective-permute-start(bf16[12,2,8,1408]{3,2,1,0:T(8,128)(2,1)S(1)} %get-tuple-element.130), channel_id=1, source_target_pairs={{0,8},{4,12},{8,0},{12,4},{1,9},{5,13},{9,1},{13,5},{2,10},{6,14},... | collective-permute-start | bytes 1622024 | tf_op jit(solution)/shard_map/ppermute | solution.py:186
  36.3 43.5 %collective-permute-start.5 = (bf16[12,2,8,1408]{3,2,1,0:T(8,128)(2,1)S(1)}, bf16[12,2,8,1408]{3,2,1,0:T(8,128)(2,1)S(1)}, u32[]{:S(2)}, u32[]{:S(2)}) collective-permute-start(bf16[12,2,8,1408]{3,2,1,0:T(8,128)(2,1)S(1)} %get-tuple-element.129), channel_id=1, source_target_pairs={{0,12},{4,0},{8,4},{12,8},{1,13},{5,1},{9,5},{13,9},{2,14},{6,2},{... | collective-permute-start | bytes 1622024 | tf_op jit(solution)/shard_map/ppermute | solution.py:186
  36.4 25.9 %collective-permute-start.10 = (bf16[12,2,8,1408]{3,2,1,0:T(8,128)(2,1)S(1)}, bf16[12,2,8,1408]{3,2,1,0:T(8,128)(2,1)S(1)}, u32[]{:S(2)}, u32[]{:S(2)}) collective-permute-start(bf16[12,2,8,1408]{3,2,1,0:T(8,128)(2,1)S(1)} %get-tuple-element.133), channel_id=1, source_target_pairs={{0,12},{4,0},{8,4},{12,8},{1,13},{5,1},{9,5},{13,9},{2,14},{6,2},{... | collective-permute-start | bytes 1622024 | tf_op jit(solution)/shard_map/ppermute | solution.py:186
  36.8 25.6 %collective-permute-start.8 = (bf16[12,2,8,1408]{3,2,1,0:T(8,128)(2,1)S(1)}, bf16[12,2,8,1408]{3,2,1,0:T(8,128)(2,1)S(1)}, u32[]{:S(2)}, u32[]{:S(2)}) collective-permute-start(bf16[12,2,8,1408]{3,2,1,0:T(8,128)(2,1)S(1)} %get-tuple-element.135), channel_id=1, source_target_pairs={{0,4},{4,8},{8,12},{12,0},{1,5},{5,9},{9,13},{13,1},{2,6},{6,10},{... | collective-permute-start | bytes 1622024 | tf_op jit(solution)/shard_map/ppermute | solution.py:186
  38.2 24.8 %collective-permute-start.9 = (bf16[12,2,8,1408]{3,2,1,0:T(8,128)(2,1)S(1)}, bf16[12,2,8,1408]{3,2,1,0:T(8,128)(2,1)S(1)}, u32[]{:S(2)}, u32[]{:S(2)}) collective-permute-start(bf16[12,2,8,1408]{3,2,1,0:T(8,128)(2,1)S(1)} %get-tuple-element.134), channel_id=1, source_target_pairs={{0,8},{4,12},{8,0},{12,4},{1,9},{5,13},{9,1},{13,5},{2,10},{6,14},... | collective-permute-start | bytes 1622024 | tf_op jit(solution)/shard_map/ppermute | solution.py:186
  62.3 22.5 %collective-permute-start.14 = (bf16[12,2,8,1408]{3,2,1,0:T(8,128)(2,1)S(1)}, bf16[12,2,8,1408]{3,2,1,0:T(8,128)(2,1)S(1)}, u32[]{:S(2)}, u32[]{:S(2)}) collective-permute-start(bf16[12,2,8,1408]{3,2,1,0:T(8,128)(2,1)S(1)} %get-tuple-element.127), channel_id=1, source_target_pairs={{0,4},{4,8},{8,12},{12,0},{1,5},{5,9},{9,13},{13,1},{2,6},{6,10},{... | collective-permute-start | bytes 1622024 | tf_op jit(solution)/shard_map/ppermute | solution.py:186
  62.3 23.8 %collective-permute-start.15 = (bf16[12,2,8,1408]{3,2,1,0:T(8,128)(2,1)S(1)}, bf16[12,2,8,1408]{3,2,1,0:T(8,128)(2,1)S(1)}, u32[]{:S(2)}, u32[]{:S(2)}) collective-permute-start(bf16[12,2,8,1408]{3,2,1,0:T(8,128)(2,1)S(1)} %get-tuple-element.126), channel_id=1, source_target_pairs={{0,8},{4,12},{8,0},{12,4},{1,9},{5,13},{9,1},{13,5},{2,10},{6,14},... | collective-permute-start | bytes 1622024 | tf_op jit(solution)/shard_map/ppermute | solution.py:186
  63.0 28.8 %collective-permute-start.16 = (bf16[12,2,8,1408]{3,2,1,0:T(8,128)(2,1)S(1)}, bf16[12,2,8,1408]{3,2,1,0:T(8,128)(2,1)S(1)}, u32[]{:S(2)}, u32[]{:S(2)}) collective-permute-start(bf16[12,2,8,1408]{3,2,1,0:T(8,128)(2,1)S(1)} %get-tuple-element.125), channel_id=1, source_target_pairs={{0,12},{4,0},{8,4},{12,8},{1,13},{5,1},{9,5},{13,9},{2,14},{6,2},{... | collective-permute-start | bytes 1622024 | tf_op jit(solution)/shard_map/ppermute | solution.py:186
  76.6 20.3 %collective-permute-start.11 = (bf16[8,2,8,1408]{3,2,1,0:T(8,128)(2,1)S(1)}, bf16[8,2,8,1408]{3,2,1,0:T(8,128)(2,1)S(1)}, u32[]{:S(2)}, u32[]{:S(2)}) collective-permute-start(bf16[8,2,8,1408]{3,2,1,0:T(8,128)(2,1)S(1)} %get-tuple-element.114), channel_id=1, source_target_pairs={{0,1},{1,2},{2,3},{4,5},{5,6},{6,7},{8,9},{9,10},{10,11},{12,13},{... | collective-permute-start | bytes 1081352 | tf_op jit(solution)/shard_map/ppermute | solution.py:18
  81.7 25.6 %collective-permute-start.6 = (bf16[8,2,8,1408]{3,2,1,0:T(8,128)(2,1)S(1)}, bf16[8,2,8,1408]{3,2,1,0:T(8,128)(2,1)S(1)}, u32[]{:S(2)}, u32[]{:S(2)}) collective-permute-start(bf16[8,2,8,1408]{3,2,1,0:T(8,128)(2,1)S(1)} %get-tuple-element.111), channel_id=1, source_target_pairs={{0,1},{1,2},{2,3},{4,5},{5,6},{6,7},{8,9},{9,10},{10,11},{12,13},{... | collective-permute-start | bytes 1081352 | tf_op jit(solution)/shard_map/ppermute | solution.py:18
  84.9 22.6 %collective-permute-start.7 = (bf16[8,2,8,1408]{3,2,1,0:T(8,128)(2,1)S(1)}, bf16[8,2,8,1408]{3,2,1,0:T(8,128)(2,1)S(1)}, u32[]{:S(2)}, u32[]{:S(2)}) collective-permute-start(bf16[8,2,8,1408]{3,2,1,0:T(8,128)(2,1)S(1)} %get-tuple-element.112), channel_id=1, source_target_pairs={{1,0},{2,1},{3,2},{5,4},{6,5},{7,6},{9,8},{10,9},{11,10},{13,12},{... | collective-permute-start | bytes 1081352 | tf_op jit(solution)/shard_map/ppermute | solution.py:18
  86.2 17.5 %collective-permute-start.12 = (bf16[8,2,8,1408]{3,2,1,0:T(8,128)(2,1)S(1)}, bf16[8,2,8,1408]{3,2,1,0:T(8,128)(2,1)S(1)}, u32[]{:S(2)}, u32[]{:S(2)}) collective-permute-start(bf16[8,2,8,1408]{3,2,1,0:T(8,128)(2,1)S(1)} %get-tuple-element.115), channel_id=1, source_target_pairs={{1,0},{2,1},{3,2},{5,4},{6,5},{7,6},{9,8},{10,9},{11,10},{13,12},{... | collective-permute-start | bytes 1081352 | tf_op jit(solution)/shard_map/ppermute | solution.py:18
  93.6 16.5 %collective-permute-start.17 = (bf16[8,2,8,1408]{3,2,1,0:T(8,128)(2,1)S(1)}, bf16[8,2,8,1408]{3,2,1,0:T(8,128)(2,1)S(1)}, u32[]{:S(2)}, u32[]{:S(2)}) collective-permute-start(bf16[8,2,8,1408]{3,2,1,0:T(8,128)(2,1)S(1)} %get-tuple-element.117), channel_id=1, source_target_pairs={{0,1},{1,2},{2,3},{4,5},{5,6},{6,7},{8,9},{9,10},{10,11},{12,13},{... | collective-permute-start | bytes 1081352 | tf_op jit(solution)/shard_map/ppermute | solution.py:18
  96.9 14.5 %collective-permute-start.18 = (bf16[8,2,8,1408]{3,2,1,0:T(8,128)(2,1)S(1)}, bf16[8,2,8,1408]{3,2,1,0:T(8,128)(2,1)S(1)}, u32[]{:S(2)}, u32[]{:S(2)}) collective-permute-start(bf16[8,2,8,1408]{3,2,1,0:T(8,128)(2,1)S(1)} %get-tuple-element.118), channel_id=1, source_target_pairs={{1,0},{2,1},{3,2},{5,4},{6,5},{7,6},{9,8},{10,9},{11,10},{13,12},{... | collective-permute-start | bytes 1081352 | tf_op jit(solution)/shard_map/ppermute | solution.py:18
  103.9 8.0 %collective-permute-start.13 = (bf16[16,2,8,128]{3,2,1,0:T(8,128)(2,1)S(1)}, bf16[16,2,8,128]{3,2,1,0:T(8,128)(2,1)S(1)}, u32[]{:S(2)}, u32[]{:S(2)}) collective-permute-start(bf16[16,2,8,128]{3,2,1,0:T(8,128)(2,1)S(1)} %slice.402), channel_id=1, source_target_pairs={{0,4},{4,8},{8,12},{1,5},{5,9},{9,13},{2,6},{6,10},{10,14},{3,7},{... | collective-permute-start | bytes 196616 | tf_op jit(solution)/shard_map/ppermute | solution.py:18
  107.6 5.6 %collective-permute-start.19 = (bf16[16,2,8,128]{3,2,1,0:T(8,128)(2,1)S(1)}, bf16[16,2,8,128]{3,2,1,0:T(8,128)(2,1)S(1)}, u32[]{:S(2)}, u32[]{:S(2)}) collective-permute-start(bf16[16,2,8,128]{3,2,1,0:T(8,128)(2,1)S(1)} %slice.401), channel_id=1, source_target_pairs={{4,0},{8,4},{12,8},{5,1},{9,5},{13,9},{6,2},{10,6},{14,10},{7,3},{... | collective-permute-start | bytes 196616 | tf_op jit(solution)/shard_map/ppermute | solution.py:18
